TPU v7x, 128 devices: a whole 4x4x4 slice. The times are simulated.
128 devices in a mesh: dp: 4 (over z_hi, core), point: 32 (over x, z_lo, y).
Axes of the slice: x: 4, y: 4, z: 4 (z_hi: 2, z_lo: 2; z = z_hi * 2 + z_lo), core: 2. Of those that a mesh axis runs over, the one named last changes fastest.
Arguments:
- points: bfloat16 [1048576, 256], P(('dp', 'point')), parts along dimension 0, may hold values from -6 to 6
- tree_order: int32 [1048576], P(('dp', 'point')), parts along dimension 0, may hold values from 0 to 262143, as said below
- ball_counts: int32 [4096], P(('dp', 'point')), parts along dimension 0, may hold values from 64 to 256, as said below
- ball_proj: bfloat16 [3, 256, 256], replicated
- ball_out: bfloat16 [256, 256], replicated, may hold values from -0.375 to 0.375
- pool_weight: bfloat16 [16384, 256], replicated, may hold values from -0.046875 to 0.046875
- coarse_proj: bfloat16 [3, 256, 256], replicated
- coarse_out: bfloat16 [256, 256], replicated, may hold values from -6 to 6
- global_proj: bfloat16 [3, 256, 256], replicated
- global_out: bfloat16 [256, 256], replicated, may hold values from -6 to 6
- unpool_weight: bfloat16 [256, 16384], replicated, may hold values from -0.125 to 0.125
- mlp_in: bfloat16 [256, 1024], replicated, may hold values from -0.375 to 0.375
- mlp_out: bfloat16 [1024, 256], replicated, may hold values from -0.1875 to 0.1875
Outputs:
- result: bfloat16 [1048576, 256], P(('dp', 'point')), parts along dimension 0
There are 4 independent parts, one for each index of `dp`. A program takes and returns all parts, laid end to end along the dimension named above; an argument that names none is the same for every part. Nothing has to cross between parts.
Inputs may be any that keep to these rules, and one draw needn't show every extreme that they name: `tree_order`: each block of 8192 slots takes a permutation of the same block of rows. `ball_counts`: live points come first in each ball; every block of 8192 slots holds a full ball.
All inputs are finite; a program needn't handle non-finite values.
Results may differ from a plain program's by a relative error of at most 0.03.
Values may be sent and summed in bfloat16 or wider, within the bound.
No kernel may reach another device: no remote copies, remote signals or barrier semaphores. Data moves between devices by JAX's collectives and lax.ppermute only.
A program may use at most 256 MiB of HBM per device.

v0:
```python
import math

import jax
import jax.numpy as jnp
from jax import lax
from jax.sharding import PartitionSpec as P

HEADS = 8
BALL = 256
POOL = 64


EPSILON = 1e-05


def partner(shard, axis, apart):
    return lax.ppermute(shard, axis, [(i, i ^ 1 << apart) for i in range(lax.axis_size(axis))])


def normalize(inputs):
    inputs = inputs.astype(jnp.float32)
    center = inputs - jnp.mean(inputs, axis=-1, keepdims=True)
    spread = jnp.mean(center * center, axis=-1, keepdims=True)
    return (center * lax.rsqrt(spread + EPSILON)).astype(jnp.bfloat16)


def project(inputs, weight):
    return jnp.dot(inputs, weight, preferred_element_type=jnp.float32).astype(jnp.bfloat16)


def attend(queries, key_rows, value_rows, valid, head_count):
    groups, q_rows, feature = queries.shape
    k_rows = key_rows.shape[1]
    head_size = feature // head_count
    q_heads = queries.reshape(groups, q_rows, head_count, head_size)
    k_heads = key_rows.reshape(groups, k_rows, head_count, head_size)
    v_heads = value_rows.reshape(groups, k_rows, head_count, head_size)
    scores = jnp.einsum(
        "bqhd,bkhd->bhqk", q_heads, k_heads, preferred_element_type=jnp.float32
    ) / math.sqrt(head_size)
    if valid is not None:
        scores = jnp.where(valid[:, None, None, :], scores, -1e30)
    row_max = jnp.max(scores, axis=-1, keepdims=True)
    expo = jnp.exp(scores - row_max)
    attn_probs = (expo / jnp.sum(expo, axis=-1, keepdims=True)).astype(jnp.bfloat16)
    mixed = jnp.einsum("bhqk,bkhd->bqhd", attn_probs, v_heads, preferred_element_type=jnp.float32)
    return mixed.reshape(groups, q_rows, feature).astype(jnp.bfloat16)


def ball_section(tree_rows, live_mask, ball_proj, ball_out):
    row_count, feature = tree_rows.shape
    normed = normalize(tree_rows)
    queries = project(normed, ball_proj[0])
    key_rows = project(normed, ball_proj[1])
    value_rows = project(normed, ball_proj[2])
    groups = row_count // BALL
    mixed = attend(
        queries.reshape(groups, BALL, feature),
        key_rows.reshape(groups, BALL, feature),
        value_rows.reshape(groups, BALL, feature),
        live_mask.reshape(groups, BALL),
        HEADS,
    )
    fine = tree_rows.astype(jnp.float32) + jnp.dot(
        mixed.reshape(row_count, feature), ball_out, preferred_element_type=jnp.float32
    )
    return fine.astype(jnp.bfloat16)


def fine_section(tree_rows, live_mask, ball_proj, ball_out, pool_weight, mlp_in, mlp_out):
    row_count, feature = tree_rows.shape
    fine = ball_section(tree_rows, live_mask, ball_proj, ball_out)
    masked = jnp.where(live_mask[:, None], fine, jnp.zeros((), jnp.bfloat16))
    pooled = jnp.dot(
        masked.reshape(row_count // POOL, POOL * feature),
        pool_weight,
        preferred_element_type=jnp.float32,
    )
    expanded = jax.nn.gelu(
        jnp.dot(normalize(fine), mlp_in, preferred_element_type=jnp.float32), approximate=True
    ).astype(jnp.bfloat16)
    refined = fine.astype(jnp.float32) + jnp.dot(
        expanded, mlp_out, preferred_element_type=jnp.float32
    )
    return (pooled, refined)


def coarse_qkv(coarse_state, weights):
    normed = normalize(coarse_state)
    return (project(normed, weights[0]), project(normed, weights[1]), project(normed, weights[2]))


def coarse_update(coarse_state, queries, key_rows, value_rows, out_weight):
    mixed = attend(queries, key_rows, value_rows, None, HEADS)
    return coarse_state + jnp.dot(mixed, out_weight, preferred_element_type=jnp.float32)


def local(
    points,
    tree_order,
    ball_counts,
    ball_proj,
    ball_out,
    pool_weight,
    coarse_proj,
    coarse_out,
    global_proj,
    global_out,
    unpool_weight,
    mlp_in,
    mlp_out,
):
    row_count, feature = points.shape
    offset = lax.axis_index("point") * row_count
    tree_rows = jnp.take(points, tree_order - offset, axis=0)
    live_mask = (jnp.arange(BALL, dtype=jnp.int32)[None, :] < ball_counts[:, None]).reshape(-1)
    pooled, refined = fine_section(
        tree_rows, live_mask, ball_proj, ball_out, pool_weight, mlp_in, mlp_out
    )
    device_count = lax.axis_size("point")
    level_count = device_count.bit_length() - 1
    coarse_state = pooled[None]
    for level_index in range(level_count):
        queries, key_rows, value_rows = coarse_qkv(coarse_state, coarse_proj)
        received = partner(jnp.stack([key_rows, value_rows]), "point", level_index)
        coarse_state = coarse_update(
            coarse_state,
            queries,
            jnp.concatenate([key_rows, received[0]], axis=1),
            jnp.concatenate([value_rows, received[1]], axis=1),
            coarse_out,
        )
    queries, key_rows, value_rows = coarse_qkv(coarse_state, global_proj)
    all_keys, all_values = (
        lax.all_gather(key_rows, "point", axis=1, tiled=True),
        lax.all_gather(value_rows, "point", axis=1, tiled=True),
    )
    mixed = attend(queries, all_keys, all_values, None, HEADS)
    summary = (
        coarse_state + jnp.dot(mixed, global_out, preferred_element_type=jnp.float32)
    ).astype(jnp.bfloat16)
    unpooled = jnp.dot(
        summary.reshape(-1, feature), unpool_weight, preferred_element_type=jnp.float32
    ).reshape(row_count, feature)
    total = refined + unpooled
    return jnp.where(live_mask[:, None], total, 0.0).astype(jnp.bfloat16)


def solution(mesh):
    placed = (
        P(("dp", "point"), None),
        P(("dp", "point")),
        P(("dp", "point")),
        P(),
        P(),
        P(),
        P(),
        P(),
        P(),
        P(),
        P(),
        P(),
        P(),
    )
    return jax.shard_map(
        local, mesh=mesh, in_specs=placed, out_specs=P(("dp", "point"), None), check_vma=False
    )
```

profile of v0, /device:TPU:0, one launch (start us, length us, event | category | flops | bytes accessed | tf_op | source)
XLA Modules:
  0.0 618.3 jit_solution(15861133291099284663)
XLA Ops:
  6.5 0.8 fusion.186
  7.4 0.8 compare_and_fusion
  8.2 33.9 %gather_fusion = bf16[8192,256]{1,0:T(8,128)(2,1)} fusion(bf16[8192,256]{1,0:T(8,128)(2,1)} %param.13, s32[8192]{0:T(1024)S(1)} %fusion.186), kind=kCustom, calls=%fused_computation | custom fusion | bytes 8421376 | tf_op jit(solution)/shard_map/jit(_take)/gather | solution.py:115
  42.0 6.4 %copy.49 = bf16[8192,256]{0,1:T(8,128)(2,1)} copy(bf16[8192,256]{1,0:T(8,128)(2,1)} %gather_fusion) | data formatting | bytes 8388608 | tf_op jit(solution)/shard_map/jit(_take)/gather | solution.py:115
  48.4 3.2 convert_reduce_fusion.1
  51.9 1.4 fusion.45
  53.3 3.9 convolution_convert_fusion.1
  57.2 3.9 convolution_convert_fusion
  61.1 3.8 convolution_convert_fusion.2
  65.0 6.3 %copy.51 = bf16[8192,256]{0,1:T(8,128)(2,1)} copy(bf16[8192,256]{1,0:T(8,128)(2,1)} %convolution_convert_fusion.1) | data formatting | bytes 8388608 | tf_op jit(solution)/shard_map/convert_element_type | solution.py:28
  71.3 5.5 copy.93
  76.8 6.4 %copy.52 = bf16[8192,256]{0,1:T(8,128)(2,1)} copy(bf16[8192,256]{1,0:T(8,128)(2,1)} %convolution_convert_fusion) | data formatting | bytes 8388608 | tf_op jit(solution)/shard_map/convert_element_type | solution.py:28
  83.2 5.6 copy.94
  88.9 6.5 %copy.50 = bf16[8192,256]{0,1:T(8,128)(2,1)} copy(bf16[8192,256]{1,0:T(8,128)(2,1)} %convolution_convert_fusion.2) | data formatting | bytes 8388608 | tf_op jit(solution)/shard_map/convert_element_type | solution.py:28
  95.4 5.5 copy.92
  101.0 33.8 %fusion.267 = (f32[32,8,256]{2,1,0:T(8,128)S(1)}, f32[32,8,256,256]{2,3,1,0:T(8,128)}) fusion(pred[32,256]{1,0:T(8,128)(4,1)S(1)} %iota_compare_fusion, bf16[32,256,8,32]{1,0,3,2:T(8,128)(2,1)} %bitcast.213, bf16[32,256,8,32]{1,0,3,2:T(8,128)(2,1)} %bitcast.212), kind=kOutput, calls=%fused_computation.278 | convolution fusion | flops 1140850944 | bytes 75767808 | tf_op jit(solution)/shard_map/sub | solution.py:44
  134.8 26.2 %convert_bitcast_fusion = bf16[32,256,8,32]{1,3,2,0:T(8,128)(2,1)} fusion(f32[32,8,256,256]{2,3,1,0:T(8,128)} %get-tuple-element.16, f32[32,8,256]{2,1,0:T(8,128)S(1)} %get-tuple-element.15, bf16[32,256,8,32]{1,0,3,2:T(8,128)(2,1)} %bitcast.214), kind=kOutput, calls=%fused_computation.58 | convolution fusion | flops 1109393408 | bytes 75759616 | tf_op jit(solution)/shard_map/bhqk,bkhd->bqhd/dot_general | solution.py:46
  161.0 4.8 copy.57
  165.8 4.4 copy.95
  170.2 4.5 broadcast_select_fusion.1
  174.7 6.4 %copy.59 = bf16[8192,256]{1,0:T(8,128)(2,1)} copy(bf16[8192,256]{0,1:T(8,128)(2,1)} %get-tuple-element.17) | data formatting | bytes 8388608 | tf_op jit(solution)/shard_map/jit(_where)/select_n | solution.py:73
  181.1 7.4 %reshape.607 = bf16[128,16384]{1,0:T(8,128)(2,1)} reshape(bf16[8192,256]{1,0:T(8,128)(2,1)} %copy.59) | data formatting | bytes 8388608 | tf_op jit(solution)/shard_map/reshape | solution.py:75
  188.4 6.0 fusion.276
  195.1 2.2 collective-permute-start
  197.8 3.0 collective-permute-done
  201.1 0.7 fusion.277
  201.7 0.8 convolution_convert_fusion.7
  202.5 0.3 fusion.280
  203.7 3.4 collective-permute-start.1
  207.4 2.8 collective-permute-done.1
  210.5 0.7 fusion.281
  211.2 0.8 convolution_convert_fusion.6
  211.9 0.3 fusion.284
  213.2 2.2 collective-permute-start.2
  215.6 2.7 collective-permute-done.2
  218.5 0.6 fusion.285
  219.2 0.8 convolution_convert_fusion.5
  220.0 0.3 fusion.288
  221.2 1.7 collective-permute-start.3
  223.2 3.1 collective-permute-done.3
  226.5 0.7 fusion.289
  227.2 0.8 convolution_convert_fusion.4
  227.9 0.3 fusion.292
  229.2 3.2 collective-permute-start.4
  232.7 3.1 collective-permute-done.4
  236.0 0.7 fusion.293
  236.6 0.8 convolution_convert_fusion.3
  237.4 0.3 fusion.296
  238.0 0.8 convolution_convert_fusion.8
  238.9 0.8 convolution_convert_fusion.10
  239.7 3.0 convert_reduce_fusion
  242.8 0.4 copy-done.3
  243.2 1.1 fusion.43
  244.6 149.4 %all-gather.7.cloned.1.call-done = bf16[4096,256]{1,0:T(8,128)(2,1)} async-done(((bf16[128,256]{1,0:T(8,128)(2,1)}), bf16[4096,256]{1,0:T(8,128)(2,1)}) %all-gather.7.cloned.1.call-update) | async-done | bytes 2097168 | tf_op jit(solution)/shard_map/all_gather | solution.py:135
  394.0 3.1 copy.87
  397.1 8.4 %fusion.297 = (f32[8,128]{1,0:T(8,128)S(1)}, f32[8,128,4096]{2,1,0:T(8,128)}) fusion(bf16[128,8,32]{0,2,1:T(8,128)(2,1)S(1)} %bitcast.254, bf16[4096,8,32]{0,2,1:T(8,128)(2,1)S(1)} %bitcast.216), kind=kOutput, calls=%fused_computation.290 | convolution fusion | flops 281022464 | bytes 18944000 | tf_op jit(solution)/shard_map/sub | solution.py:44
  405.5 142.9 %all-gather.5.cloned.1.call-done = bf16[4096,256]{1,0:T(8,128)(2,1)} async-done(((bf16[128,256]{1,0:T(8,128)(2,1)}), bf16[4096,256]{1,0:T(8,128)(2,1)}) %all-gather.5.cloned.1.call-update) | async-done | bytes 2097168 | tf_op jit(solution)/shard_map/all_gather | solution.py:136
  548.4 2.9 copy.85
  551.3 8.8 %fusion.86 = bf16[8,32,128]{2,1,0:T(8,128)(2,1)S(1)} fusion(bf16[4096,8,32]{0,2,1:T(8,128)(2,1)S(1)} %bitcast.217, f32[8,128,4096]{2,1,0:T(8,128)} %get-tuple-element.32, f32[8,128]{1,0:T(8,128)S(1)} %get-tuple-element.31), kind=kOutput, calls=%fused_computation.88 | convolution fusion | flops 276856832 | bytes 18944000 | tf_op jit(solution)/shard_map/bhqk,bkhd->bqhd/dot_general | solution.py:46
  560.1 8.1 %fusion.88 = f32[128,16384]{1,0:T(8,128)} fusion(bf16[256,16384]{1,0:T(8,128)(2,1)} %param.23, f32[128,256]{1,0:T(8,128)S(1)} %get-tuple-element.30, bf16[128,256]{0,1:T(8,128)(2,1)S(1)} %bitcast.228, bf16[256,256]{1,0:T(8,128)(2,1)S(1)} %copy-done.7), kind=kOutput, calls=%fused_computation.113 | convolution fusion | flops 1090584576 | bytes 17104896 | tf_op jit(solution)/shard_map/dot_general | solution.py:142
  568.2 9.3 %reshape.621 = f32[8192,256]{1,0:T(8,128)} reshape(f32[128,16384]{1,0:T(8,128)} %fusion.88) | data formatting | bytes 16777216 | tf_op jit(solution)/shard_map/reshape | solution.py:144
  577.5 9.0 %copy.88 = f32[8192,256]{0,1:T(8,128)} copy(f32[8192,256]{1,0:T(8,128)} %reshape.621) | data formatting | bytes 16777216 | tf_op jit(solution)/shard_map/reshape | solution.py:144
  586.5 18.4 %fusion.33 = bf16[8192,256]{0,1:T(8,128)(2,1)} fusion(f32[8192,256]{0,1:T(8,128)} %copy.88, bf16[1024,256]{1,0:T(8,128)(2,1)S(1)} %copy-done, bf16[8192,256]{0,1:T(8,128)(2,1)} %get-tuple-element.18, bf16[256,1024]{1,0:T(8,128)(2,1)S(1)} %copy-done.9, f32[8192]{0:T(1024)S(1)} %add_rsqrt_fusion, f32[8192]{0:T(1024)S(1)} %broadcast_multiply_fusion, ...), kind=kOutput, calls=%fused_computation.38 | convolution fusion | flops 8684306432 | bytes 17899520 | tf_op jit(solution)/shard_map/dot_general | solution.py:82
  604.9 6.4 %copy.89 = bf16[8192,256]{1,0:T(8,128)(2,1)} copy(bf16[8192,256]{0,1:T(8,128)(2,1)} %fusion.33) | data formatting | bytes 8388608 | tf_op jit(solution)/shard_map/convert_element_type | solution.py:146
  (109 shorter events, 7.9 us)
Async XLA Ops:
  6.5 579.9 %copy-start = (bf16[1024,256]{1,0:T(8,128)(2,1)S(1)}, bf16[1024,256]{1,0:T(8,128)(2,1)}, u32[]{:S(2)}) copy-start(bf16[1024,256]{1,0:T(8,128)(2,1)} %param.25) | copy-start | bytes 1572868
  6.5 387.5 %all-gather.7.cloned.1.call-start = ((), (), s32[]{:S(2)}) async-start(), calls=%async_computation.1 | async-start | bytes 2162688 | tf_op jit(solution)/shard_map/all_gather | solution.py:135
  48.4 3.4 copy-start.1
  48.4 4.9 copy-start.10
  83.2 5.6 copy-start.8
  165.8 4.4 copy-start.2
  165.8 4.4 copy-start.11
  188.4 6.4 %copy-start.4 = (bf16[3,256,256]{2,1,0:T(8,128)(2,1)S(1)}, bf16[3,256,256]{2,1,0:T(8,128)(2,1)}, u32[]{:S(2)}) copy-start(bf16[3,256,256]{2,1,0:T(8,128)(2,1)} %param.19) | copy-start | bytes 1179652
  194.4 8.0 %copy-start.5 = (bf16[256,256]{1,0:T(8,128)(2,1)S(1)}, bf16[256,256]{1,0:T(8,128)(2,1)}, u32[]{:S(2)}) copy-start(bf16[256,256]{1,0:T(8,128)(2,1)} %param.20) | copy-start | bytes 393220
  195.1 5.7 collective-permute-start
  203.7 6.6 %collective-permute-start.1 = (bf16[2,1,128,256]{3,2,1,0:T(8,128)(2,1)S(1)}, bf16[2,1,128,256]{3,2,1,0:T(8,128)(2,1)S(1)}, u32[]{:S(2)}, u32[]{:S(2)}) collective-permute-start(bf16[2,1,128,256]{3,2,1,0:T(8,128)(2,1)S(1)} %pad_maximum_fusion.1), channel_id=1, source_target_pairs={{0,2},{1,3},{2,0},{3,1},{4,6},{5,7},{6,4},{7,5},{8,10},{9,11},{10,... | collective-permute-start | bytes 393224 | tf_op jit(solution)/shard_map/ppermute | solution.py:17
  213.2 5.1 collective-permute-start.2
  221.2 5.0 collective-permute-start.3
  228.9 9.1 %copy-start.6 = (bf16[3,256,256]{2,1,0:T(8,128)(2,1)S(1)}, bf16[3,256,256]{2,1,0:T(8,128)(2,1)}, u32[]{:S(2)}) copy-start(bf16[3,256,256]{2,1,0:T(8,128)(2,1)} %param.21) | copy-start | bytes 1179652
  229.2 6.6 %collective-permute-start.4 = (bf16[2,1,128,256]{3,2,1,0:T(8,128)(2,1)S(1)}, bf16[2,1,128,256]{3,2,1,0:T(8,128)(2,1)S(1)}, u32[]{:S(2)}, u32[]{:S(2)}) collective-permute-start(bf16[2,1,128,256]{3,2,1,0:T(8,128)(2,1)S(1)} %pad_maximum_fusion.4), channel_id=1, source_target_pairs={{0,16},{1,17},{2,18},{3,19},{4,20},{5,21},{6,22},{7,23},{8,24},{9,... | collective-permute-start | bytes 393224 | tf_op jit(solution)/shard_map/ppermute | solution.py:17
  238.9 309.5 %all-gather.5.cloned.1.call-start = ((), (), s32[]{:S(2)}) async-start(), calls=%async_computation | async-start | bytes 2162688 | tf_op jit(solution)/shard_map/all_gather | solution.py:136
  239.7 3.5 copy-start.3
  551.3 8.8 %copy-start.7 = (bf16[256,256]{1,0:T(8,128)(2,1)S(1)}, bf16[256,256]{1,0:T(8,128)(2,1)}, u32[]{:S(2)}) copy-start(bf16[256,256]{1,0:T(8,128)(2,1)} %param.22) | copy-start | bytes 393220
  577.5 9.0 %copy-start.9 = (bf16[256,1024]{1,0:T(8,128)(2,1)S(1)}, bf16[256,1024]{1,0:T(8,128)(2,1)}, u32[]{:S(2)}) copy-start(bf16[256,1024]{1,0:T(8,128)(2,1)} %param.24) | copy-start | bytes 1572868
Sparse Core Ops, SparseCore 0:
  239.0 154.9 all-gather.6
  395.7 152.6 all-gather.4
where the time goes:
time: 629 us; the launch traced here: 618 us
  waiting for transfers between devices  307 us (49%)
  matrix products  139 us (22%)
  local copies, waits for them, and re-layouts  133 us (21%)
  between operations  14.3 us (2%)
  starting transfers between devices  12.7 us (2%)
  other arithmetic  12.4 us (2%)
    all_gather x1, waiting for transfers between devices, local(): lax.all_gather(key_rows, 'point', axis=1, tiled=True)  149 us
    all_gather x1, waiting for transfers between devices, local(): lax.all_gather(value_rows, 'point', axis=1, tiled=True)  143 us
    sub x7, matrix products, attend(): expo = jnp.exp(scores - row_max)  45.4 us
    gather x2, local copies, waits for them, and re-layouts, local(): tree_rows = jnp.take(points, tree_order - offset, axis=0)  40.3 us
    dot_general x7, matrix products, attend(): jnp.einsum('bhqk,bkhd->bqhd', attn_probs, v_heads, preferred_element_type...  38.9 us
    unnamed x28, local copies, waits for them, and re-layouts  21.6 us
    convert_element_type x19, local copies, waits for them, and re-layouts, project(): jnp.dot(inputs, weight, preferred_element_type=jnp.float32)  21.1 us
    dot_general x1, matrix products, fine_section(): jnp.dot(expanded, mlp_out, preferred_element_type=jnp.float32)  18.4 us
  transfers between devices with their start and end apart: 7, of which 7 were waited for; matrix products, arithmetic and copies ran while one was open for 3% of the time, Pallas kernels for 0%

commit v1 on v0

--- a/solution.py
+++ b/solution.py
@@ -3,6 +3,8 @@
 import jax
 import jax.numpy as jnp
 from jax import lax
+from jax.experimental import pallas as pl
+from jax.experimental.pallas import tpu as pltpu
 from jax.sharding import PartitionSpec as P
 
 HEADS = 8
@@ -11,6 +13,74 @@
 
 
 EPSILON = 1e-05
+GATHER_ORDER = (1, 4, 0, 2, 3)
+
+
+def _norm(x):
+    center = x - jnp.mean(x, axis=-1, keepdims=True)
+    spread = jnp.mean(center * center, axis=-1, keepdims=True)
+    return (center * lax.rsqrt(spread + EPSILON)).astype(jnp.bfloat16)
+
+
+def _ball_kernel(counts_ref, x_ref, proj_ref, wo_ref, w1_ref, w2_ref, masked_ref, refined_ref):
+    count = counts_ref[pl.program_id(0)]
+    x = x_ref[...].astype(jnp.float32)
+    feature = x.shape[-1]
+    head_size = feature // HEADS
+    normed = _norm(x)
+    q = jnp.dot(normed, proj_ref[0], preferred_element_type=jnp.float32).astype(jnp.bfloat16)
+    k = jnp.dot(normed, proj_ref[1], preferred_element_type=jnp.float32).astype(jnp.bfloat16)
+    v = jnp.dot(normed, proj_ref[2], preferred_element_type=jnp.float32).astype(jnp.bfloat16)
+    key_live = lax.broadcasted_iota(jnp.int32, (1, BALL), 1) < count
+    lane = lax.broadcasted_iota(jnp.int32, (1, feature), 1)
+    scale = 1.0 / math.sqrt(head_size)
+    mixed = jnp.zeros((BALL, feature), jnp.float32)
+    for h in range(HEADS):
+        in_head = (lane >= h * head_size) & (lane < (h + 1) * head_size)
+        qh = jnp.where(in_head, q, jnp.zeros((), jnp.bfloat16))
+        vh = jnp.where(in_head, v, jnp.zeros((), jnp.bfloat16))
+        scores = lax.dot_general(qh, k, (((1,), (1,)), ((), ())), preferred_element_type=jnp.float32) * scale
+        scores = jnp.where(key_live, scores, -1e30)
+        row_max = jnp.max(scores, axis=-1, keepdims=True)
+        expo = jnp.exp(scores - row_max)
+        probs = (expo * (1.0 / jnp.sum(expo, axis=-1, keepdims=True))).astype(jnp.bfloat16)
+        mixed = mixed + jnp.dot(probs, vh, preferred_element_type=jnp.float32)
+    mixed = mixed.astype(jnp.bfloat16)
+    fine = (x + jnp.dot(mixed, wo_ref[...], preferred_element_type=jnp.float32)).astype(jnp.bfloat16)
+    row_live = lax.broadcasted_iota(jnp.int32, (BALL, 1), 0) < count
+    masked_ref[...] = jnp.where(row_live, fine, jnp.zeros((), jnp.bfloat16))
+    hidden = jnp.dot(_norm(fine.astype(jnp.float32)), w1_ref[...], preferred_element_type=jnp.float32)
+    hidden = jax.nn.gelu(hidden, approximate=True).astype(jnp.bfloat16)
+    refined_ref[...] = fine.astype(jnp.float32) + jnp.dot(hidden, w2_ref[...], preferred_element_type=jnp.float32)
+
+
+def ball_block(tree_rows, ball_counts, ball_proj, ball_out, mlp_in, mlp_out):
+    rows, feature = tree_rows.shape
+    ff = mlp_in.shape[1]
+    balls = rows // BALL
+    const2 = lambda i, c: (0, 0)
+    return pl.pallas_call(
+        _ball_kernel,
+        out_shape=(jax.ShapeDtypeStruct((rows, feature), jnp.bfloat16),
+                   jax.ShapeDtypeStruct((rows, feature), jnp.float32)),
+        grid_spec=pltpu.PrefetchScalarGridSpec(
+            num_scalar_prefetch=1, grid=(balls,),
+            in_specs=[pl.BlockSpec((BALL, feature), lambda i, c: (i, 0)),
+                      pl.BlockSpec((3, feature, feature), lambda i, c: (0, 0, 0)),
+                      pl.BlockSpec((feature, feature), const2),
+                      pl.BlockSpec((feature, ff), const2),
+                      pl.BlockSpec((ff, feature), const2)],
+            out_specs=[pl.BlockSpec((BALL, feature), lambda i, c: (i, 0)),
+                       pl.BlockSpec((BALL, feature), lambda i, c: (i, 0))]),
+        compiler_params=pltpu.CompilerParams(dimension_semantics=("arbitrary",)),
+    )(ball_counts, tree_rows, ball_proj, ball_out, mlp_in, mlp_out)
+
+
+def gather_all(shard, axis, order):
+    gathered = shard
+    for apart in order:
+        gathered = jnp.concatenate([gathered, partner(gathered, axis, apart)], axis=0)
+    return gathered
 
 
 def partner(shard, axis, apart):
@@ -45,44 +115,6 @@
     attn_probs = (expo / jnp.sum(expo, axis=-1, keepdims=True)).astype(jnp.bfloat16)
     mixed = jnp.einsum("bhqk,bkhd->bqhd", attn_probs, v_heads, preferred_element_type=jnp.float32)
     return mixed.reshape(groups, q_rows, feature).astype(jnp.bfloat16)
-
-
-def ball_section(tree_rows, live_mask, ball_proj, ball_out):
-    row_count, feature = tree_rows.shape
-    normed = normalize(tree_rows)
-    queries = project(normed, ball_proj[0])
-    key_rows = project(normed, ball_proj[1])
-    value_rows = project(normed, ball_proj[2])
-    groups = row_count // BALL
-    mixed = attend(
-        queries.reshape(groups, BALL, feature),
-        key_rows.reshape(groups, BALL, feature),
-        value_rows.reshape(groups, BALL, feature),
-        live_mask.reshape(groups, BALL),
-        HEADS,
-    )
-    fine = tree_rows.astype(jnp.float32) + jnp.dot(
-        mixed.reshape(row_count, feature), ball_out, preferred_element_type=jnp.float32
-    )
-    return fine.astype(jnp.bfloat16)
-
-
-def fine_section(tree_rows, live_mask, ball_proj, ball_out, pool_weight, mlp_in, mlp_out):
-    row_count, feature = tree_rows.shape
-    fine = ball_section(tree_rows, live_mask, ball_proj, ball_out)
-    masked = jnp.where(live_mask[:, None], fine, jnp.zeros((), jnp.bfloat16))
-    pooled = jnp.dot(
-        masked.reshape(row_count // POOL, POOL * feature),
-        pool_weight,
-        preferred_element_type=jnp.float32,
-    )
-    expanded = jax.nn.gelu(
-        jnp.dot(normalize(fine), mlp_in, preferred_element_type=jnp.float32), approximate=True
-    ).astype(jnp.bfloat16)
-    refined = fine.astype(jnp.float32) + jnp.dot(
-        expanded, mlp_out, preferred_element_type=jnp.float32
-    )
-    return (pooled, refined)
 
 
 def coarse_qkv(coarse_state, weights):
@@ -114,8 +146,11 @@
     offset = lax.axis_index("point") * row_count
     tree_rows = jnp.take(points, tree_order - offset, axis=0)
     live_mask = (jnp.arange(BALL, dtype=jnp.int32)[None, :] < ball_counts[:, None]).reshape(-1)
-    pooled, refined = fine_section(
-        tree_rows, live_mask, ball_proj, ball_out, pool_weight, mlp_in, mlp_out
+    masked, refined = ball_block(tree_rows, ball_counts, ball_proj, ball_out, mlp_in, mlp_out)
+    pooled = jnp.dot(
+        masked.reshape(row_count // POOL, POOL * feature),
+        pool_weight,
+        preferred_element_type=jnp.float32,
     )
     device_count = lax.axis_size("point")
     level_count = device_count.bit_length() - 1
@@ -131,10 +166,8 @@
             coarse_out,
         )
     queries, key_rows, value_rows = coarse_qkv(coarse_state, global_proj)
-    all_keys, all_values = (
-        lax.all_gather(key_rows, "point", axis=1, tiled=True),
-        lax.all_gather(value_rows, "point", axis=1, tiled=True),
-    )
+    both = gather_all(jnp.concatenate([key_rows[0], value_rows[0]], axis=1), "point", GATHER_ORDER)
+    all_keys, all_values = both[None, :, :feature], both[None, :, feature:]
     mixed = attend(queries, all_keys, all_values, None, HEADS)
     summary = (
         coarse_state + jnp.dot(mixed, global_out, preferred_element_type=jnp.float32)

time: 629 us -> 331 us (0.53); the launches traced: 618 us -> 330 us
  waiting for transfers between devices: 307 us -> 78 us
  matrix products: 139 us -> 44 us
  Pallas kernels: 0 us -> 93.8 us
  local copies, waits for them, and re-layouts: 133 us -> 69.9 us
  between operations: 14.3 us -> 0.66 us
  starting transfers between devices: 12.7 us -> 24.3 us
  other arithmetic: 12.4 us -> 19.7 us
    all_gather x2 -> x0, waiting for transfers between devices: 292 us -> none  [the longest x1 149 us: local(): lax.all_gather(key_rows, 'point', axis=1, tiled=True)]
    pallas_call x0 -> x1, Pallas kernels: none -> 93.8 us  [ball_block(): pl.pallas_call(_ball_kernel, out_shape=(jax.ShapeDtypeStruct((rows, featu...]
    ppermute x5 -> x10, waiting for transfers between devices: 14.6 us -> 78 us  [partner(): lax.ppermute(shard, axis, [(i, i ^ 1 << apart) for i in range(lax.axis_si...]
    sub x7 -> x6, matrix products: 45.4 us -> 13 us  [attend(): expo = jnp.exp(scores - row_max)]
    dot_general x7 -> x6, matrix products: 38.9 us -> 12.6 us  [attend(): jnp.einsum('bhqk,bkhd->bqhd', attn_probs, v_heads, preferred_element_type...]
    dot_general x3 -> x1, matrix products: 28.9 us -> 6.02 us  [local(): jnp.dot(masked.reshape(row_count // POOL, POOL * feature), pool_weight, p...]
    convert_element_type x19 -> x16, local copies, waits for them, and re-layouts: 21.1 us -> 1.84 us  [project(): jnp.dot(inputs, weight, preferred_element_type=jnp.float32)]
    unnamed x28 -> x15, local copies, waits for them, and re-layouts: 21.6 us -> 2.61 us
  transfers between devices with their start and end apart: 7 -> 10, of which waited for: 7 -> 10; matrix products, arithmetic and copies ran while one was open for 3% -> 1% of each run, Pallas kernels for 0% -> 0%
where the time goes in v1:
time: 331 us; the launch traced here: 330 us
  Pallas kernels  93.8 us (28%)
  waiting for transfers between devices  78 us (24%)
  local copies, waits for them, and re-layouts  69.9 us (21%)
  matrix products  44 us (13%)
  starting transfers between devices  24.3 us (7%)
  other arithmetic  19.7 us (6%)
    pallas_call x1, Pallas kernels, ball_block(): pl.pallas_call(_ball_kernel, out_shape=(jax.ShapeDtypeStruct((rows, featu...  93.8 us
    ppermute x10, waiting for transfers between devices, partner(): lax.ppermute(shard, axis, [(i, i ^ 1 << apart) for i in range(lax.axis_si...  78 us
    gather x1, local copies, waits for them, and re-layouts, local(): tree_rows = jnp.take(points, tree_order - offset, axis=0)  33.9 us
    ppermute x10, starting transfers between devices, partner(): lax.ppermute(shard, axis, [(i, i ^ 1 << apart) for i in range(lax.axis_si...  24.3 us
    sub x6, matrix products, attend(): expo = jnp.exp(scores - row_max)  13 us
    dot_general x6, matrix products, attend(): jnp.einsum('bhqk,bkhd->bqhd', attn_probs, v_heads, preferred_element_type...  12.6 us
    slice x3, local copies, waits for them, and re-layouts, local(): all_keys, all_values = (both[None, :, :feature], both[None, :, feature:])  10.8 us
    convert_element_type x1, other arithmetic, local(): return jnp.where(live_mask[:, None], total, 0.0).astype(jnp.bfloat16)  10.1 us
  transfers between devices with their start and end apart: 10, of which 10 were waited for; matrix products, arithmetic and copies ran while one was open for 1% of the time, Pallas kernels for 0%

profile of v1, /device:TPU:0, one launch (start us, length us, event | category | flops | bytes accessed | tf_op | source)
XLA Modules:
  0.0 330.3 jit_solution(10611488328161234766)
XLA Ops:
  0.0 0.8 fusion.117
  0.8 0.8 compare_and_fusion
  1.6 33.9 %gather_fusion = bf16[8192,256]{1,0:T(8,128)(2,1)} fusion(bf16[8192,256]{1,0:T(8,128)(2,1)} %param.13, s32[8192]{0:T(1024)S(1)} %fusion.117), kind=kCustom, calls=%fused_computation | custom fusion | bytes 8421376 | tf_op jit(solution)/shard_map/jit(_take)/gather | solution.py:147
  35.5 5.2 %broadcast_select_fusion.x_ref = bf16[8192,256]{1,0:T(8,128)(2,1)} fusion(bf16[8192,256]{1,0:T(8,128)(2,1)} %gather_fusion, pred[8192]{0:T(1024)(128)(4,1)S(1)} %compare_and_fusion), kind=kLoop, calls=%fused_computation.14 | loop fusion | flops 2097152 | bytes 8396800 | tf_op jit(solution)/shard_map/jit(_take)/select_n | solution.py:147
  40.7 93.8 %shard_map.127 = (bf16[8192,256]{1,0:T(8,128)(2,1)}, f32[8192,256]{1,0:T(8,128)}) custom-call(s32[32]{0:T(128)} %counts_ref.1, bf16[8192,256]{1,0:T(8,128)(2,1)} %broadcast_select_fusion.x_ref, bf16[3,256,256]{2,1,0:T(8,128)(2,1)} %proj_ref.1, bf16[256,256]{1,0:T(8,128)(2,1)} %wo_ref.1, bf16[256,1024]{1,0:T(8,128)(2,1)} %w1_ref.1, bf16[1024,256]{1,0:T(8,128)(2,1)} %w2_ref.1), custom_call_target="tpu_custom_call" | custom-call | tf_op jit(solution)/shard_map/pallas_call | solution.py:62
  134.5 7.4 %reshape.562 = bf16[128,16384]{1,0:T(8,128)(2,1)} reshape(bf16[8192,256]{1,0:T(8,128)(2,1)} %get-tuple-element.8) | data formatting | bytes 8388608 | tf_op jit(solution)/shard_map/reshape | solution.py:151
  141.8 6.0 %fusion.190 = (f32[128]{0:T(128)S(1)}, f32[128,256]{1,0:T(8,128)S(1)}) fusion(bf16[128,16384]{1,0:T(8,128)(2,1)} %reshape.562, bf16[16384,256]{1,0:T(8,128)(2,1)} %param.18), kind=kOutput, calls=%fused_computation.224 | convolution fusion | flops 1073774464 | bytes 12714496 | tf_op jit(solution)/shard_map/dot_general | solution.py:150
  147.9 0.2 multiply_reduce_fusion.6
  148.6 1.8 collective-permute-start
  150.9 3.0 collective-permute-done
  154.1 0.7 fusion.191
  154.7 0.8 convolution_convert_fusion.4
  155.5 0.3 fusion.194
  155.8 0.2 multiply_reduce_fusion.5
  156.8 3.4 %collective-permute-start.1 = (bf16[2,1,128,256]{3,2,1,0:T(8,128)(2,1)S(1)}, bf16[2,1,128,256]{3,2,1,0:T(8,128)(2,1)S(1)}, u32[]{:S(2)}, u32[]{:S(2)}) collective-permute-start(bf16[2,1,128,256]{3,2,1,0:T(8,128)(2,1)S(1)} %pad_maximum_fusion.4), channel_id=1, source_target_pairs={{0,2},{1,3},{2,0},{3,1},{4,6},{5,7},{6,4},{7,5},{8,10},{9,11},{10,... | collective-permute-start | bytes 393224 | tf_op jit(solution)/shard_map/ppermute | solution.py:87
  160.5 2.8 collective-permute-done.1
  163.6 0.7 fusion.195
  164.2 0.8 convolution_convert_fusion.3
  165.0 0.3 fusion.198
  165.3 0.2 multiply_reduce_fusion.4
  166.2 2.1 collective-permute-start.2
  168.6 2.7 collective-permute-done.2
  171.6 0.7 fusion.199
  172.2 0.8 convolution_convert_fusion.2
  173.0 0.3 fusion.202
  173.3 0.2 multiply_reduce_fusion.3
  173.8 0.2 convolution_convert_fusion.12
  174.2 1.9 collective-permute-start.3
  176.4 3.1 collective-permute-done.3
  179.7 0.7 fusion.203
  180.4 0.8 convolution_convert_fusion.1
  181.1 0.3 fusion.206
  181.4 0.2 multiply_reduce_fusion.2
  181.9 0.2 convolution_convert_fusion.9
  182.4 3.2 collective-permute-start.4
  185.9 3.1 collective-permute-done.4
  189.2 0.7 fusion.207
  189.8 0.8 convolution_convert_fusion
  190.6 0.3 fusion.210
  190.9 0.2 multiply_reduce_fusion.1
  191.6 0.7 constant_dynamic-update-slice_fusion.4
  192.3 3.3 %collective-permute-start.5 = (bf16[128,512]{1,0:T(8,128)(2,1)S(1)}, bf16[128,512]{1,0:T(8,128)(2,1)S(1)}, u32[]{:S(2)}, u32[]{:S(2)}) collective-permute-start(bf16[128,512]{1,0:T(8,128)(2,1)S(1)} %get-tuple-element.21), channel_id=1, source_target_pairs={{0,2},{1,3},{2,0},{3,1},{4,6},{5,7},{6,4},{7,5},{8,10},{9,11},{10,... | collective-permute-start | bytes 393224 | tf_op jit(solution)/shard_map/ppermute | solution.py:87
  195.6 3.2 collective-permute-done.5
  198.8 3.2 collective-permute-start.6
  202.0 4.8 %collective-permute-done.6 = bf16[256,512]{1,0:T(8,128)(2,1)S(1)} collective-permute-done((bf16[256,512]{1,0:T(8,128)(2,1)S(1)}, bf16[256,512]{1,0:T(8,128)(2,1)S(1)}, u32[]{:S(2)}, u32[]{:S(2)}) %collective-permute-start.6) | collective-permute-done | bytes 262176 | tf_op jit(solution)/shard_map/ppermute | solution.py:87
  206.8 1.8 collective-permute-start.7
  208.6 7.5 %collective-permute-done.7 = bf16[512,512]{1,0:T(8,128)(2,1)S(1)} collective-permute-done((bf16[512,512]{1,0:T(8,128)(2,1)S(1)}, bf16[512,512]{1,0:T(8,128)(2,1)S(1)}, u32[]{:S(2)}, u32[]{:S(2)}) %collective-permute-start.7) | collective-permute-done | bytes 524320 | tf_op jit(solution)/shard_map/ppermute | solution.py:87
  216.1 2.1 collective-permute-start.8
  218.2 0.7 constant_dynamic-update-slice_fusion.3
  219.0 0.8 constant_dynamic-update-slice_fusion.2
  219.8 1.0 constant_dynamic-update-slice_fusion.1
  220.8 11.7 %collective-permute-done.8 = bf16[1024,512]{1,0:T(8,128)(2,1)S(1)} collective-permute-done((bf16[1024,512]{1,0:T(8,128)(2,1)S(1)}, bf16[1024,512]{1,0:T(8,128)(2,1)S(1)}, u32[]{:S(2)}, u32[]{:S(2)}) %collective-permute-start.8) | collective-permute-done | bytes 1048608 | tf_op jit(solution)/shard_map/ppermute | solution.py:87
  232.6 1.5 constant_dynamic-update-slice_fusion
  234.0 1.5 collective-permute-start.9
  235.9 36.3 %collective-permute-done.9 = bf16[2048,512]{1,0:T(8,128)(2,1)S(1)} collective-permute-done((bf16[2048,512]{1,0:T(8,128)(2,1)}, bf16[2048,512]{1,0:T(8,128)(2,1)S(1)}, u32[]{:S(2)}, u32[]{:S(2)}) %collective-permute-start.9) | collective-permute-done | bytes 2097184 | tf_op jit(solution)/shard_map/ppermute | solution.py:87
  272.2 1.5 constant_dynamic-update-slice_fusion.5
  273.6 3.8 %fusion.184 = (bf16[4096,256]{1,0:T(8,128)(2,1)S(1)}, bf16[4096,256]{1,0:T(8,128)(2,1)}) fusion(bf16[4096,512]{1,0:T(8,128)(2,1)} %constant_dynamic-update-slice_fusion.5), kind=kLoop, calls=%fused_computation.218 | loop fusion | bytes 8388608 | tf_op jit(solution)/shard_map/slice | solution.py:170
  277.5 4.1 %copy.67 = bf16[4096,256]{0,1:T(8,128)(2,1)} copy(bf16[4096,256]{1,0:T(8,128)(2,1)} %get-tuple-element.10) | data formatting | bytes 4194304 | tf_op jit(solution)/shard_map/slice | solution.py:170
  281.5 2.9 copy.69
  284.4 9.7 %fusion.211 = (f32[8,128]{1,0:T(8,128)S(1)}, f32[8,128,4096]{2,1,0:T(8,128)}) fusion(bf16[128,8,32]{0,2,1:T(8,128)(2,1)S(1)} %bitcast.201, bf16[4096,8,32]{0,2,1:T(8,128)(2,1)} %bitcast.174), kind=kOutput, calls=%fused_computation.235 | convolution fusion | flops 281022464 | bytes 18944000 | tf_op jit(solution)/shard_map/sub | solution.py:114
  294.1 8.8 %fusion.23 = bf16[8,32,128]{2,1,0:T(8,128)(2,1)S(1)} fusion(bf16[4096,8,32]{0,2,1:T(8,128)(2,1)S(1)} %bitcast.173, f32[8,128,4096]{2,1,0:T(8,128)} %get-tuple-element.45, f32[8,128]{1,0:T(8,128)S(1)} %get-tuple-element.44), kind=kOutput, calls=%fused_computation.37 | convolution fusion | flops 276856832 | bytes 18944000 | tf_op jit(solution)/shard_map/bhqk,bkhd->bqhd/dot_general | solution.py:116
  302.9 8.0 %fusion.25 = f32[128,16384]{1,0:T(8,128)} fusion(bf16[256,16384]{1,0:T(8,128)(2,1)} %param.23, f32[128,256]{1,0:T(8,128)S(1)} %get-tuple-element.43, bf16[128,256]{0,1:T(8,128)(2,1)S(1)} %bitcast.185, bf16[256,256]{1,0:T(8,128)(2,1)S(1)} %copy-done), kind=kOutput, calls=%fused_computation.62 | convolution fusion | flops 1090584576 | bytes 17104896 | tf_op jit(solution)/shard_map/dot_general | solution.py:175
  311.0 9.3 %reshape.576 = f32[8192,256]{1,0:T(8,128)} reshape(f32[128,16384]{1,0:T(8,128)} %fusion.25) | data formatting | bytes 16777216 | tf_op jit(solution)/shard_map/reshape | solution.py:177
  320.2 10.1 %select_convert_fusion = bf16[8192,256]{1,0:T(8,128)(2,1)} fusion(f32[8192,256]{1,0:T(8,128)} %get-tuple-element.7, f32[8192,256]{1,0:T(8,128)} %reshape.576, pred[8192]{0:T(1024)(128)(4,1)S(1)} %lt.31), kind=kLoop, calls=%fused_computation.11 | loop fusion | flops 6291456 | bytes 20979712 | tf_op jit(solution)/shard_map/convert_element_type | solution.py:179
  (87 shorter events, 6.6 us)
Async XLA Ops:
  0.0 302.9 %copy-start = (bf16[256,256]{1,0:T(8,128)(2,1)S(1)}, bf16[256,256]{1,0:T(8,128)(2,1)}, u32[]{:S(2)}) copy-start(bf16[256,256]{1,0:T(8,128)(2,1)} %param.22) | copy-start | bytes 393220
  141.8 6.4 %copy-start.1 = (bf16[3,256,256]{2,1,0:T(8,128)(2,1)S(1)}, bf16[3,256,256]{2,1,0:T(8,128)(2,1)}, u32[]{:S(2)}) copy-start(bf16[3,256,256]{2,1,0:T(8,128)(2,1)} %param.19) | copy-start | bytes 1179652
  147.9 7.6 %copy-start.2 = (bf16[256,256]{1,0:T(8,128)(2,1)S(1)}, bf16[256,256]{1,0:T(8,128)(2,1)}, u32[]{:S(2)}) copy-start(bf16[256,256]{1,0:T(8,128)(2,1)} %param.20) | copy-start | bytes 393220
  148.6 5.3 %collective-permute-start = (bf16[2,1,128,256]{3,2,1,0:T(8,128)(2,1)S(1)}, bf16[2,1,128,256]{3,2,1,0:T(8,128)(2,1)S(1)}, u32[]{:S(2)}, u32[]{:S(2)}) collective-permute-start(bf16[2,1,128,256]{3,2,1,0:T(8,128)(2,1)S(1)} %pad_maximum_fusion.3), channel_id=1, source_target_pairs={{0,1},{1,0},{2,3},{3,2},{4,5},{5,4},{6,7},{7,6},{8,9},{9,8},{10,11... | collective-permute-start | bytes 393224 | tf_op jit(solution)/shard_map/ppermute | solution.py:87
  156.8 6.6 %collective-permute-start.1 = (bf16[2,1,128,256]{3,2,1,0:T(8,128)(2,1)S(1)}, bf16[2,1,128,256]{3,2,1,0:T(8,128)(2,1)S(1)}, u32[]{:S(2)}, u32[]{:S(2)}) collective-permute-start(bf16[2,1,128,256]{3,2,1,0:T(8,128)(2,1)S(1)} %pad_maximum_fusion.4), channel_id=1, source_target_pairs={{0,2},{1,3},{2,0},{3,1},{4,6},{5,7},{6,4},{7,5},{8,10},{9,11},{10,... | collective-permute-start | bytes 393224 | tf_op jit(solution)/shard_map/ppermute | solution.py:87
  166.2 5.1 %collective-permute-start.2 = (bf16[2,1,128,256]{3,2,1,0:T(8,128)(2,1)S(1)}, bf16[2,1,128,256]{3,2,1,0:T(8,128)(2,1)S(1)}, u32[]{:S(2)}, u32[]{:S(2)}) collective-permute-start(bf16[2,1,128,256]{3,2,1,0:T(8,128)(2,1)S(1)} %pad_maximum_fusion.5), channel_id=1, source_target_pairs={{0,4},{1,5},{2,6},{3,7},{4,0},{5,1},{6,2},{7,3},{8,12},{9,13},{10,... | collective-permute-start | bytes 393224 | tf_op jit(solution)/shard_map/ppermute | solution.py:87
  174.2 5.2 %collective-permute-start.3 = (bf16[2,1,128,256]{3,2,1,0:T(8,128)(2,1)S(1)}, bf16[2,1,128,256]{3,2,1,0:T(8,128)(2,1)S(1)}, u32[]{:S(2)}, u32[]{:S(2)}) collective-permute-start(bf16[2,1,128,256]{3,2,1,0:T(8,128)(2,1)S(1)} %pad_maximum_fusion.6), channel_id=1, source_target_pairs={{0,8},{1,9},{2,10},{3,11},{4,12},{5,13},{6,14},{7,15},{8,0},{9,1},... | collective-permute-start | bytes 393224 | tf_op jit(solution)/shard_map/ppermute | solution.py:87
  182.1 9.1 %copy-start.4 = (bf16[3,256,256]{2,1,0:T(8,128)(2,1)S(1)}, bf16[3,256,256]{2,1,0:T(8,128)(2,1)}, u32[]{:S(2)}) copy-start(bf16[3,256,256]{2,1,0:T(8,128)(2,1)} %param.21) | copy-start | bytes 1179652
  182.4 6.6 %collective-permute-start.4 = (bf16[2,1,128,256]{3,2,1,0:T(8,128)(2,1)S(1)}, bf16[2,1,128,256]{3,2,1,0:T(8,128)(2,1)S(1)}, u32[]{:S(2)}, u32[]{:S(2)}) collective-permute-start(bf16[2,1,128,256]{3,2,1,0:T(8,128)(2,1)S(1)} %pad_maximum_fusion.7), channel_id=1, source_target_pairs={{0,16},{1,17},{2,18},{3,19},{4,20},{5,21},{6,22},{7,23},{8,24},{9,... | collective-permute-start | bytes 393224 | tf_op jit(solution)/shard_map/ppermute | solution.py:87
  192.3 6.5 %collective-permute-start.5 = (bf16[128,512]{1,0:T(8,128)(2,1)S(1)}, bf16[128,512]{1,0:T(8,128)(2,1)S(1)}, u32[]{:S(2)}, u32[]{:S(2)}) collective-permute-start(bf16[128,512]{1,0:T(8,128)(2,1)S(1)} %get-tuple-element.21), channel_id=1, source_target_pairs={{0,2},{1,3},{2,0},{3,1},{4,6},{5,7},{6,4},{7,5},{8,10},{9,11},{10,... | collective-permute-start | bytes 393224 | tf_op jit(solution)/shard_map/ppermute | solution.py:87
  198.8 8.0 %collective-permute-start.6 = (bf16[256,512]{1,0:T(8,128)(2,1)S(1)}, bf16[256,512]{1,0:T(8,128)(2,1)S(1)}, u32[]{:S(2)}, u32[]{:S(2)}) collective-permute-start(bf16[256,512]{1,0:T(8,128)(2,1)S(1)} %pad_maximum_fusion.2), channel_id=1, source_target_pairs={{0,16},{1,17},{2,18},{3,19},{4,20},{5,21},{6,22},{7,23},{8,24},{9,... | collective-permute-start | bytes 786440 | tf_op jit(solution)/shard_map/ppermute | solution.py:87
  206.8 28.7 %copy-start.5 = (s32[32]{0:T(128)S(1)}, s32[32]{0:T(128)}, u32[]{:S(2)}) copy-start(s32[32]{0:T(128)} %counts_ref.1) | copy-start | bytes 388
  206.8 9.3 %collective-permute-start.7 = (bf16[512,512]{1,0:T(8,128)(2,1)S(1)}, bf16[512,512]{1,0:T(8,128)(2,1)S(1)}, u32[]{:S(2)}, u32[]{:S(2)}) collective-permute-start(bf16[512,512]{1,0:T(8,128)(2,1)S(1)} %pad_maximum_fusion.1), channel_id=1, source_target_pairs={{0,1},{1,0},{2,3},{3,2},{4,5},{5,4},{6,7},{7,6},{8,9},{9,8},{10,11... | collective-permute-start | bytes 1572872 | tf_op jit(solution)/shard_map/ppermute | solution.py:87
  216.1 16.4 %collective-permute-start.8 = (bf16[1024,512]{1,0:T(8,128)(2,1)S(1)}, bf16[1024,512]{1,0:T(8,128)(2,1)S(1)}, u32[]{:S(2)}, u32[]{:S(2)}) collective-permute-start(bf16[1024,512]{1,0:T(8,128)(2,1)S(1)} %pad_maximum_fusion), channel_id=1, source_target_pairs={{0,4},{1,5},{2,6},{3,7},{4,0},{5,1},{6,2},{7,3},{8,12},{9,13},{10,... | collective-permute-start | bytes 3145736 | tf_op jit(solution)/shard_map/ppermute | solution.py:87
  234.0 38.1 %collective-permute-start.9 = (bf16[2048,512]{1,0:T(8,128)(2,1)}, bf16[2048,512]{1,0:T(8,128)(2,1)S(1)}, u32[]{:S(2)}, u32[]{:S(2)}) collective-permute-start(bf16[2048,512]{1,0:T(8,128)(2,1)} %get-tuple-element.11), channel_id=1, source_target_pairs={{0,8},{1,9},{2,10},{3,11},{4,12},{5,13},{6,14},{7,15},{8,0},{9,1},... | collective-permute-start | bytes 6291464 | tf_op jit(solution)/shard_map/ppermute | solution.py:87
  284.4 9.7 %copy-start.3 = (bf16[4096,256]{0,1:T(8,128)(2,1)S(1)}, bf16[4096,256]{0,1:T(8,128)(2,1)}, u32[]{:S(2)}) copy-start(bf16[4096,256]{0,1:T(8,128)(2,1)} %copy.67) | copy-start | bytes 6291460

commit v2 on v1

--- a/solution.py
+++ b/solution.py
@@ -7,6 +7,7 @@
 from jax.experimental.pallas import tpu as pltpu
 from jax.sharding import PartitionSpec as P
 
+
 HEADS = 8
 BALL = 256
 POOL = 64
@@ -14,6 +15,7 @@
 
 EPSILON = 1e-05
 GATHER_ORDER = (1, 4, 0, 2, 3)
+MLP_CHUNK_ROWS = 1024
 
 
 def _norm(x):
@@ -22,7 +24,7 @@
     return (center * lax.rsqrt(spread + EPSILON)).astype(jnp.bfloat16)
 
 
-def _ball_kernel(counts_ref, x_ref, proj_ref, wo_ref, w1_ref, w2_ref, masked_ref, refined_ref):
+def _ball_kernel(counts_ref, x_ref, proj_ref, wo_ref, masked_ref):
     count = counts_ref[pl.program_id(0)]
     x = x_ref[...].astype(jnp.float32)
     feature = x.shape[-1]
@@ -49,37 +51,51 @@
     fine = (x + jnp.dot(mixed, wo_ref[...], preferred_element_type=jnp.float32)).astype(jnp.bfloat16)
     row_live = lax.broadcasted_iota(jnp.int32, (BALL, 1), 0) < count
     masked_ref[...] = jnp.where(row_live, fine, jnp.zeros((), jnp.bfloat16))
-    hidden = jnp.dot(_norm(fine.astype(jnp.float32)), w1_ref[...], preferred_element_type=jnp.float32)
-    hidden = jax.nn.gelu(hidden, approximate=True).astype(jnp.bfloat16)
-    refined_ref[...] = fine.astype(jnp.float32) + jnp.dot(hidden, w2_ref[...], preferred_element_type=jnp.float32)
-
-
-def ball_block(tree_rows, ball_counts, ball_proj, ball_out, mlp_in, mlp_out):
+
+
+def ball_block(tree_rows, ball_counts, ball_proj, ball_out):
     rows, feature = tree_rows.shape
-    ff = mlp_in.shape[1]
     balls = rows // BALL
-    const2 = lambda i, c: (0, 0)
     return pl.pallas_call(
         _ball_kernel,
-        out_shape=(jax.ShapeDtypeStruct((rows, feature), jnp.bfloat16),
-                   jax.ShapeDtypeStruct((rows, feature), jnp.float32)),
+        out_shape=jax.ShapeDtypeStruct((rows, feature), jnp.bfloat16),
         grid_spec=pltpu.PrefetchScalarGridSpec(
             num_scalar_prefetch=1, grid=(balls,),
             in_specs=[pl.BlockSpec((BALL, feature), lambda i, c: (i, 0)),
                       pl.BlockSpec((3, feature, feature), lambda i, c: (0, 0, 0)),
-                      pl.BlockSpec((feature, feature), const2),
-                      pl.BlockSpec((feature, ff), const2),
-                      pl.BlockSpec((ff, feature), const2)],
-            out_specs=[pl.BlockSpec((BALL, feature), lambda i, c: (i, 0)),
-                       pl.BlockSpec((BALL, feature), lambda i, c: (i, 0))]),
+                      pl.BlockSpec((feature, feature), lambda i, c: (0, 0))],
+            out_specs=pl.BlockSpec((BALL, feature), lambda i, c: (i, 0))),
         compiler_params=pltpu.CompilerParams(dimension_semantics=("arbitrary",)),
-    )(ball_counts, tree_rows, ball_proj, ball_out, mlp_in, mlp_out)
+    )(ball_counts, tree_rows, ball_proj, ball_out)
+
+
+def _mlp_kernel(fine_ref, w1_ref, w2_ref, refined_ref):
+    fine = fine_ref[...]
+    hidden = jnp.dot(_norm(fine.astype(jnp.float32)), w1_ref[...], preferred_element_type=jnp.float32)
+    hidden = jax.nn.gelu(hidden, approximate=True).astype(jnp.bfloat16)
+    refined_ref[...] = fine.astype(jnp.float32) + jnp.dot(hidden, w2_ref[...], preferred_element_type=jnp.float32)
+
+
+def mlp_block(fine, mlp_in, mlp_out):
+    rows, feature = fine.shape
+    ff = mlp_in.shape[1]
+    return pl.pallas_call(
+        _mlp_kernel,
+        out_shape=jax.ShapeDtypeStruct((rows, feature), jnp.float32),
+        grid=(rows // BALL,),
+        in_specs=[pl.BlockSpec((BALL, feature), lambda i: (i, 0)),
+                  pl.BlockSpec((feature, ff), lambda i: (0, 0)),
+                  pl.BlockSpec((ff, feature), lambda i: (0, 0))],
+        out_specs=pl.BlockSpec((BALL, feature), lambda i: (i, 0)),
+        compiler_params=pltpu.CompilerParams(dimension_semantics=("arbitrary",)),
+    )(fine, mlp_in, mlp_out)
 
 
 def gather_all(shard, axis, order):
     gathered = shard
     for apart in order:
-        gathered = jnp.concatenate([gathered, partner(gathered, axis, apart)], axis=0)
+        received = partner(gathered, axis, apart)
+        gathered = jnp.concatenate([gathered, received], axis=0)
     return gathered
 
 
@@ -127,7 +143,7 @@
     return coarse_state + jnp.dot(mixed, out_weight, preferred_element_type=jnp.float32)
 
 
-def local(
+def local_body(
     points,
     tree_order,
     ball_counts,
@@ -146,7 +162,11 @@
     offset = lax.axis_index("point") * row_count
     tree_rows = jnp.take(points, tree_order - offset, axis=0)
     live_mask = (jnp.arange(BALL, dtype=jnp.int32)[None, :] < ball_counts[:, None]).reshape(-1)
-    masked, refined = ball_block(tree_rows, ball_counts, ball_proj, ball_out, mlp_in, mlp_out)
+    masked = ball_block(tree_rows, ball_counts, ball_proj, ball_out)
+    chunk = MLP_CHUNK_ROWS
+    refined_parts = []
+    for start in range(0, row_count, chunk):
+        refined_parts.append(mlp_block(masked[start:start + chunk], mlp_in, mlp_out))
     pooled = jnp.dot(
         masked.reshape(row_count // POOL, POOL * feature),
         pool_weight,
@@ -165,9 +185,12 @@
             jnp.concatenate([value_rows, received[1]], axis=1),
             coarse_out,
         )
-    queries, key_rows, value_rows = coarse_qkv(coarse_state, global_proj)
-    both = gather_all(jnp.concatenate([key_rows[0], value_rows[0]], axis=1), "point", GATHER_ORDER)
-    all_keys, all_values = both[None, :, :feature], both[None, :, feature:]
+    normed = normalize(coarse_state)
+    queries = project(normed, global_proj[0])
+    everyone = gather_all(coarse_state[0].astype(jnp.bfloat16), "point", GATHER_ORDER)[None]
+    normed_all = normalize(everyone)
+    all_keys = project(normed_all, global_proj[1])
+    all_values = project(normed_all, global_proj[2])
     mixed = attend(queries, all_keys, all_values, None, HEADS)
     summary = (
         coarse_state + jnp.dot(mixed, global_out, preferred_element_type=jnp.float32)
@@ -175,7 +198,7 @@
     unpooled = jnp.dot(
         summary.reshape(-1, feature), unpool_weight, preferred_element_type=jnp.float32
     ).reshape(row_count, feature)
-    total = refined + unpooled
+    total = jnp.concatenate(refined_parts, axis=0) + unpooled
     return jnp.where(live_mask[:, None], total, 0.0).astype(jnp.bfloat16)
 
 
@@ -195,6 +218,4 @@
         P(),
         P(),
     )
-    return jax.shard_map(
-        local, mesh=mesh, in_specs=placed, out_specs=P(("dp", "point"), None), check_vma=False
-    )
+    return jax.shard_map(local_body, mesh=mesh, in_specs=placed, out_specs=P(("dp", "point"), None), check_vma=False)

time: 331 us -> 317 us (0.958)
  waiting for transfers between devices: 78 us -> 42.4 us
  Pallas kernels: 93.8 us -> 106 us
  matrix products: 44 us -> 48.7 us
  local copies, waits for them, and re-layouts: 69.9 us -> 74 us
    ppermute x10, waiting for transfers between devices: 78 us -> 42.4 us  [partner(): lax.ppermute(shard, axis, [(i, i ^ 1 << apart) for i in range(lax.axis_si...]
    pallas_call x1 -> x9, Pallas kernels: 93.8 us -> 106 us  [the longest x1 63.3 us: ball_block(): pl.pallas_call(_ball_kernel, out_shape=jax.ShapeDtypeStruct((rows, featur...]
    unnamed x15 -> x42, local copies, waits for them, and re-layouts: 2.61 us -> 15 us
    slice x18 -> x16, local copies, waits for them, and re-layouts: 12 us -> 5.43 us  [the longest x1 4.25 us: local_body(): masked[start:start + chunk]]
    dot_general x18, matrix products: 2.86 us -> 8.41 us  [project(): jnp.dot(inputs, weight, preferred_element_type=jnp.float32)]
  transfers between devices with their start and end apart: 10 -> 10, of which waited for: 10 -> 9; matrix products, arithmetic and copies ran while one was open for 1% -> 7% of each run, Pallas kernels for 0% -> 14%
where the time goes in v2:
time: 317 us; the launch traced here: 315 us
  Pallas kernels  106 us (33%)
  local copies, waits for them, and re-layouts  74 us (23%)
  matrix products  48.7 us (15%)
  waiting for transfers between devices  42.4 us (13%)
  starting transfers between devices  22.2 us (7%)
  other arithmetic  20.8 us (7%)
    pallas_call x1, Pallas kernels, ball_block(): pl.pallas_call(_ball_kernel, out_shape=jax.ShapeDtypeStruct((rows, featur...  63.3 us
    pallas_call x8, Pallas kernels, mlp_block(): pl.pallas_call(_mlp_kernel, out_shape=jax.ShapeDtypeStruct((rows, feature...  43.1 us
    ppermute x10, waiting for transfers between devices, partner(): lax.ppermute(shard, axis, [(i, i ^ 1 << apart) for i in range(lax.axis_si...  42.4 us
    gather x1, local copies, waits for them, and re-layouts, local_body(): tree_rows = jnp.take(points, tree_order - offset, axis=0)  33.9 us
    ppermute x10, starting transfers between devices, partner(): lax.ppermute(shard, axis, [(i, i ^ 1 << apart) for i in range(lax.axis_si...  22.2 us
    unnamed x42, local copies, waits for them, and re-layouts  15 us
    dot_general x6, matrix products, attend(): jnp.einsum('bhqk,bkhd->bqhd', attn_probs, v_heads, preferred_element_type...  13.2 us
    sub x6, matrix products, attend(): expo = jnp.exp(scores - row_max)  11.6 us
  transfers between devices with their start and end apart: 10, of which 9 were waited for; matrix products, arithmetic and copies ran while one was open for 7% of the time, Pallas kernels for 14%

profile of v2, /device:TPU:0, one launch (start us, length us, event | category | flops | bytes accessed | tf_op | source)
XLA Modules:
  0.0 315.3 jit_solution(5048459648270183034)
XLA Ops:
  0.0 0.8 fusion.122
  0.8 0.8 compare_and_fusion
  1.6 33.9 %gather_fusion = bf16[8192,256]{1,0:T(8,128)(2,1)} fusion(bf16[8192,256]{1,0:T(8,128)(2,1)} %param.13, s32[8192]{0:T(1024)S(1)} %fusion.122), kind=kCustom, calls=%fused_computation | custom fusion | bytes 8421376 | tf_op jit(solution)/shard_map/jit(_take)/gather | solution.py:163
  35.5 5.2 %broadcast_select_fusion.x_ref = bf16[8192,256]{1,0:T(8,128)(2,1)} fusion(bf16[8192,256]{1,0:T(8,128)(2,1)} %gather_fusion, pred[8192]{0:T(1024)(128)(4,1)S(1)} %compare_and_fusion), kind=kLoop, calls=%fused_computation.21 | loop fusion | flops 2097152 | bytes 8396800 | tf_op jit(solution)/shard_map/jit(_take)/select_n | solution.py:163
  40.7 63.3 %shard_map.127 = bf16[8192,256]{1,0:T(8,128)(2,1)} custom-call(s32[32]{0:T(128)} %counts_ref.1, bf16[8192,256]{1,0:T(8,128)(2,1)} %broadcast_select_fusion.x_ref, bf16[3,256,256]{2,1,0:T(8,128)(2,1)} %proj_ref.1, bf16[256,256]{1,0:T(8,128)(2,1)} %wo_ref.1), custom_call_target="tpu_custom_call" | custom-call | tf_op jit(solution)/shard_map/pallas_call | solution.py:59
  104.1 7.4 %reshape.996 = bf16[128,16384]{1,0:T(8,128)(2,1)} reshape(bf16[8192,256]{1,0:T(8,128)(2,1)} %shard_map.127) | data formatting | bytes 8388608 | tf_op jit(solution)/shard_map/reshape | solution.py:171
  111.4 6.0 %fusion.197 = (f32[128]{0:T(128)S(1)}, f32[128,256]{1,0:T(8,128)S(1)}) fusion(bf16[128,16384]{1,0:T(8,128)(2,1)} %reshape.996, bf16[16384,256]{1,0:T(8,128)(2,1)} %param.18), kind=kOutput, calls=%fused_computation.247 | convolution fusion | flops 1073774464 | bytes 12714496 | tf_op jit(solution)/shard_map/dot_general | solution.py:170
  118.1 1.9 collective-permute-start
  120.5 4.2 %fusion.191 = (bf16[1024,256]{1,0:T(8,128)(2,1)}, bf16[1024,256]{1,0:T(8,128)(2,1)}, bf16[1024,256]{1,0:T(8,128)(2,1)}, bf16[1024,256]{1,0:T(8,128)(2,1)}, bf16[...) fusion(bf16[8192,256]{1,0:T(8,128)(2,1)} %shard_map.127), kind=kLoop, calls=%fused_computation.241 | loop fusion | bytes 8388608 | tf_op jit(solution)/shard_map/slice | solution.py:169
  125.0 5.4 %shard_map.128 = f32[1024,256]{1,0:T(8,128)} custom-call(bf16[1024,256]{1,0:T(8,128)(2,1)} %get-tuple-element.14.fine_ref, bf16[256,1024]{1,0:T(8,128)(2,1)} %w1_ref.15, bf16[1024,256]{1,0:T(8,128)(2,1)} %w2_ref.15), custom_call_target="tpu_custom_call" | custom-call | tf_op jit(solution)/shard_map/pallas_call | solution.py:82
  130.3 2.3 constant_dynamic-update-slice_fusion.7
  132.6 5.4 %shard_map.129 = f32[1024,256]{1,0:T(8,128)} custom-call(bf16[1024,256]{1,0:T(8,128)(2,1)} %get-tuple-element.13.fine_ref, bf16[256,1024]{1,0:T(8,128)(2,1)} %w1_ref.15, bf16[1024,256]{1,0:T(8,128)(2,1)} %w2_ref.15), custom_call_target="tpu_custom_call" | custom-call | tf_op jit(solution)/shard_map/pallas_call | solution.py:82
  138.0 5.4 %shard_map.130 = f32[1024,256]{1,0:T(8,128)} custom-call(bf16[1024,256]{1,0:T(8,128)(2,1)} %get-tuple-element.12.fine_ref, bf16[256,1024]{1,0:T(8,128)(2,1)} %w1_ref.15, bf16[1024,256]{1,0:T(8,128)(2,1)} %w2_ref.15), custom_call_target="tpu_custom_call" | custom-call | tf_op jit(solution)/shard_map/pallas_call | solution.py:82
  143.3 5.4 %shard_map.131 = f32[1024,256]{1,0:T(8,128)} custom-call(bf16[1024,256]{1,0:T(8,128)(2,1)} %get-tuple-element.11.fine_ref, bf16[256,1024]{1,0:T(8,128)(2,1)} %w1_ref.15, bf16[1024,256]{1,0:T(8,128)(2,1)} %w2_ref.15), custom_call_target="tpu_custom_call" | custom-call | tf_op jit(solution)/shard_map/pallas_call | solution.py:82
  148.7 5.4 %shard_map.132 = f32[1024,256]{1,0:T(8,128)} custom-call(bf16[1024,256]{1,0:T(8,128)(2,1)} %get-tuple-element.10.fine_ref, bf16[256,1024]{1,0:T(8,128)(2,1)} %w1_ref.15, bf16[1024,256]{1,0:T(8,128)(2,1)} %w2_ref.15), custom_call_target="tpu_custom_call" | custom-call | tf_op jit(solution)/shard_map/pallas_call | solution.py:82
  154.1 5.4 %shard_map.133 = f32[1024,256]{1,0:T(8,128)} custom-call(bf16[1024,256]{1,0:T(8,128)(2,1)} %get-tuple-element.9.fine_ref, bf16[256,1024]{1,0:T(8,128)(2,1)} %w1_ref.15, bf16[1024,256]{1,0:T(8,128)(2,1)} %w2_ref.15), custom_call_target="tpu_custom_call" | custom-call | tf_op jit(solution)/shard_map/pallas_call | solution.py:82
  159.4 5.4 %shard_map.134 = f32[1024,256]{1,0:T(8,128)} custom-call(bf16[1024,256]{1,0:T(8,128)(2,1)} %get-tuple-element.8.fine_ref, bf16[256,1024]{1,0:T(8,128)(2,1)} %w1_ref.15, bf16[1024,256]{1,0:T(8,128)(2,1)} %w2_ref.15), custom_call_target="tpu_custom_call" | custom-call | tf_op jit(solution)/shard_map/pallas_call | solution.py:82
  164.9 5.4 %shard_map.135 = f32[1024,256]{1,0:T(8,128)} custom-call(bf16[1024,256]{1,0:T(8,128)(2,1)} %get-tuple-element.7.fine_ref, bf16[256,1024]{1,0:T(8,128)(2,1)} %w1_ref.15, bf16[1024,256]{1,0:T(8,128)(2,1)} %w2_ref.15), custom_call_target="tpu_custom_call" | custom-call | tf_op jit(solution)/shard_map/pallas_call | solution.py:82
  170.4 2.4 constant_dynamic-update-slice_fusion.6
  172.8 2.4 constant_dynamic-update-slice_fusion.5
  175.1 1.1 constant_dynamic-update-slice_fusion.4
  176.2 1.0 constant_dynamic-update-slice_fusion.3
  177.3 1.1 constant_dynamic-update-slice_fusion.2
  178.3 1.1 constant_dynamic-update-slice_fusion.1
  179.4 1.0 constant_dynamic-update-slice_fusion
  180.7 0.6 fusion.198
  181.4 0.8 convolution_convert_fusion.6
  183.4 3.0 collective-permute-start.1
  186.6 3.3 %collective-permute-done.1 = bf16[2,1,128,256]{3,2,1,0:T(8,128)(2,1)S(1)} collective-permute-done((bf16[2,1,128,256]{3,2,1,0:T(8,128)(2,1)S(1)}, bf16[2,1,128,256]{3,2,1,0:T(8,128)(2,1)S(1)}, u32[]{:S(2)}, u32[]{:S(2)}) %collective-permute-start.1) | collective-permute-done | bytes 131104 | tf_op jit(solution)/shard_map/ppermute | solution.py:103
  190.2 0.7 fusion.202
  190.8 0.8 convolution_convert_fusion.5
  192.8 2.0 collective-permute-start.2
  195.1 2.8 collective-permute-done.2
  198.1 0.7 fusion.206
  198.8 0.8 convolution_convert_fusion.4
  200.8 1.8 collective-permute-start.3
  202.9 3.2 %collective-permute-done.3 = bf16[2,1,128,256]{3,2,1,0:T(8,128)(2,1)S(1)} collective-permute-done((bf16[2,1,128,256]{3,2,1,0:T(8,128)(2,1)S(1)}, bf16[2,1,128,256]{3,2,1,0:T(8,128)(2,1)S(1)}, u32[]{:S(2)}, u32[]{:S(2)}) %collective-permute-start.3) | collective-permute-done | bytes 131104 | tf_op jit(solution)/shard_map/ppermute | solution.py:103
  206.3 0.6 fusion.210
  207.0 0.8 convolution_convert_fusion.3
  209.0 3.1 collective-permute-start.4
  212.4 3.2 %collective-permute-done.4 = bf16[2,1,128,256]{3,2,1,0:T(8,128)(2,1)S(1)} collective-permute-done((bf16[2,1,128,256]{3,2,1,0:T(8,128)(2,1)S(1)}, bf16[2,1,128,256]{3,2,1,0:T(8,128)(2,1)S(1)}, u32[]{:S(2)}, u32[]{:S(2)}) %collective-permute-start.4) | collective-permute-done | bytes 131104 | tf_op jit(solution)/shard_map/ppermute | solution.py:103
  215.8 0.7 fusion.214
  216.4 0.8 convolution_convert_fusion.2
  217.4 3.0 collective-permute-start.5
  220.9 2.3 collective-permute-done.5
  223.3 3.1 collective-permute-start.6
  226.4 0.6 bitcast_dynamic-update-slice_fusion.11
  227.2 2.7 collective-permute-done.6
  230.9 5.4 %collective-permute-done.7 = bf16[512,256]{1,0:T(8,128)(2,1)S(1)} collective-permute-done((bf16[512,256]{1,0:T(8,128)(2,1)S(1)}, bf16[512,256]{1,0:T(8,128)(2,1)S(1)}, u32[]{:S(2)}, u32[]{:S(2)}) %collective-permute-start.7) | collective-permute-done | bytes 262176 | tf_op jit(solution)/shard_map/ppermute | solution.py:103
  236.4 2.0 collective-permute-start.8
  238.4 7.2 %collective-permute-done.8 = bf16[1024,256]{1,0:T(8,128)(2,1)S(1)} collective-permute-done((bf16[1024,256]{1,0:T(8,128)(2,1)S(1)}, bf16[1024,256]{1,0:T(8,128)(2,1)S(1)}, u32[]{:S(2)}, u32[]{:S(2)}) %collective-permute-start.8) | collective-permute-done | bytes 524320 | tf_op jit(solution)/shard_map/ppermute | solution.py:103
  245.7 1.8 collective-permute-start.9
  247.5 0.7 bitcast_dynamic-update-slice_fusion.7
  248.2 0.7 bitcast_dynamic-update-slice_fusion.5
  248.9 0.8 bitcast_dynamic-update-slice_fusion.3
  249.8 12.4 %collective-permute-done.9 = bf16[2048,256]{1,0:T(8,128)(2,1)S(1)} collective-permute-done((bf16[2048,256]{1,0:T(8,128)(2,1)S(1)}, bf16[2048,256]{1,0:T(8,128)(2,1)S(1)}, u32[]{:S(2)}, u32[]{:S(2)}) %collective-permute-start.9) | collective-permute-done | bytes 1048608 | tf_op jit(solution)/shard_map/ppermute | solution.py:103
  262.9 1.3 fusion.12
  264.3 1.9 convolution_convert_fusion
  266.2 3.9 %convolution_convert_fusion.1 = bf16[4096,256]{0,1:T(8,128)(2,1)} fusion(bf16[3,256,256]{2,1,0:T(8,128)(2,1)S(1)} %copy-done.8, bf16[1,4096,1,1,1,1,256]{6,1,5,4,3,2,0:T(8,128)(2,1)S(1)} %bitcast_dynamic-update-slice_fusion.1, f32[4096]{0:T(1024)S(1)} %add_rsqrt_fusion, f32[4096]{0:T(1024)S(1)} %broadcast_multiply_fusion), kind=kOutput, calls=%fused_computation.17 | convolution fusion | flops 542113792 | bytes 4358144 | tf_op jit(solution)/shard_map/dot_general | solution.py:114
  270.1 8.3 %fusion.217 = (f32[8,128]{1,0:T(8,128)S(1)}, f32[8,128,4096]{2,1,0:T(8,128)}) fusion(bf16[128,8,32]{0,2,1:T(8,128)(2,1)S(1)} %bitcast.210, bf16[4096,8,32]{0,2,1:T(8,128)(2,1)S(1)} %bitcast.256), kind=kOutput, calls=%fused_computation.257 | convolution fusion | flops 281022464 | bytes 18944000 | tf_op jit(solution)/shard_map/sub | solution.py:130
  278.5 9.4 %fusion.26 = bf16[8,32,128]{2,1,0:T(8,128)(2,1)S(1)} fusion(bf16[4096,8,32]{0,2,1:T(8,128)(2,1)} %bitcast.255, f32[8,128,4096]{2,1,0:T(8,128)} %get-tuple-element.37, f32[8,128]{1,0:T(8,128)S(1)} %get-tuple-element.36), kind=kOutput, calls=%fused_computation.45 | convolution fusion | flops 276856832 | bytes 18944000 | tf_op jit(solution)/shard_map/bhqk,bkhd->bqhd/dot_general | solution.py:132
  287.9 8.0 %fusion.28 = f32[128,16384]{1,0:T(8,128)} fusion(bf16[256,16384]{1,0:T(8,128)(2,1)} %param.23, f32[128,256]{1,0:T(8,128)S(1)} %get-tuple-element.35, bf16[128,256]{0,1:T(8,128)(2,1)S(1)} %bitcast.208, bf16[256,256]{1,0:T(8,128)(2,1)S(1)} %copy-done), kind=kOutput, calls=%fused_computation.68 | convolution fusion | flops 1090584576 | bytes 17104896 | tf_op jit(solution)/shard_map/dot_general | solution.py:198
  295.9 9.3 %reshape.1010 = f32[8192,256]{1,0:T(8,128)} reshape(f32[128,16384]{1,0:T(8,128)} %fusion.28) | data formatting | bytes 16777216 | tf_op jit(solution)/shard_map/reshape | solution.py:200
  305.2 10.1 %select_convert_fusion = bf16[8192,256]{1,0:T(8,128)(2,1)} fusion(f32[8192,256]{1,0:T(8,128)} %constant_dynamic-update-slice_fusion, f32[8192,256]{1,0:T(8,128)} %reshape.1010, pred[8192]{0:T(1024)(128)(4,1)S(1)} %lt.31), kind=kLoop, calls=%fused_computation.11 | loop fusion | flops 6291456 | bytes 20979712 | tf_op jit(solution)/shard_map/convert_element_type | solution.py:202
  (125 shorter events, 11.1 us)
Async XLA Ops:
  0.0 287.9 %copy-start = (bf16[256,256]{1,0:T(8,128)(2,1)S(1)}, bf16[256,256]{1,0:T(8,128)(2,1)}, u32[]{:S(2)}) copy-start(bf16[256,256]{1,0:T(8,128)(2,1)} %param.22) | copy-start | bytes 393220
  111.4 6.4 %copy-start.1 = (bf16[3,256,256]{2,1,0:T(8,128)(2,1)S(1)}, bf16[3,256,256]{2,1,0:T(8,128)(2,1)}, u32[]{:S(2)}) copy-start(bf16[3,256,256]{2,1,0:T(8,128)(2,1)} %param.19) | copy-start | bytes 1179652
  118.1 62.3 %collective-permute-start = (bf16[2,1,128,256]{3,2,1,0:T(8,128)(2,1)S(1)}, bf16[2,1,128,256]{3,2,1,0:T(8,128)(2,1)S(1)}, u32[]{:S(2)}, u32[]{:S(2)}) collective-permute-start(bf16[2,1,128,256]{3,2,1,0:T(8,128)(2,1)S(1)} %pad_maximum_fusion.2), channel_id=1, source_target_pairs={{0,1},{1,0},{2,3},{3,2},{4,5},{5,4},{6,7},{7,6},{8,9},{9,8},{10,11... | collective-permute-start | bytes 393224 | tf_op jit(solution)/shard_map/ppermute | solution.py:103
  120.5 4.3 %copy-start.9 = (s32[32]{0:T(128)S(1)}, s32[32]{0:T(128)}, u32[]{:S(2)}) copy-start(s32[32]{0:T(128)} %counts_ref.1) | copy-start | bytes 388
  159.4 15.7 %copy-start.6 = (f32[1024,256]{1,0:T(8,128)S(1)}, f32[1024,256]{1,0:T(8,128)}, u32[]{:S(2)}) copy-start(f32[1024,256]{1,0:T(8,128)} %shard_map.131) | copy-start | bytes 3145732
  164.9 11.3 %copy-start.5 = (f32[1024,256]{1,0:T(8,128)S(1)}, f32[1024,256]{1,0:T(8,128)}, u32[]{:S(2)}) copy-start(f32[1024,256]{1,0:T(8,128)} %shard_map.132) | copy-start | bytes 3145732
  170.4 6.9 %copy-start.4 = (f32[1024,256]{1,0:T(8,128)S(1)}, f32[1024,256]{1,0:T(8,128)}, u32[]{:S(2)}) copy-start(f32[1024,256]{1,0:T(8,128)} %shard_map.133) | copy-start | bytes 3145732
  172.8 5.6 %copy-start.2 = (f32[1024,256]{1,0:T(8,128)S(1)}, f32[1024,256]{1,0:T(8,128)}, u32[]{:S(2)}) copy-start(f32[1024,256]{1,0:T(8,128)} %shard_map.134) | copy-start | bytes 3145732
  175.1 4.3 %copy-start.3 = (f32[1024,256]{1,0:T(8,128)S(1)}, f32[1024,256]{1,0:T(8,128)}, u32[]{:S(2)}) copy-start(f32[1024,256]{1,0:T(8,128)} %shard_map.135) | copy-start | bytes 3145732
  179.4 2.7 copy-start.7
  183.4 6.6 %collective-permute-start.1 = (bf16[2,1,128,256]{3,2,1,0:T(8,128)(2,1)S(1)}, bf16[2,1,128,256]{3,2,1,0:T(8,128)(2,1)S(1)}, u32[]{:S(2)}, u32[]{:S(2)}) collective-permute-start(bf16[2,1,128,256]{3,2,1,0:T(8,128)(2,1)S(1)} %pad_maximum_fusion.3), channel_id=1, source_target_pairs={{0,2},{1,3},{2,0},{3,1},{4,6},{5,7},{6,4},{7,5},{8,10},{9,11},{10,... | collective-permute-start | bytes 393224 | tf_op jit(solution)/shard_map/ppermute | solution.py:103
  192.8 5.0 %collective-permute-start.2 = (bf16[2,1,128,256]{3,2,1,0:T(8,128)(2,1)S(1)}, bf16[2,1,128,256]{3,2,1,0:T(8,128)(2,1)S(1)}, u32[]{:S(2)}, u32[]{:S(2)}) collective-permute-start(bf16[2,1,128,256]{3,2,1,0:T(8,128)(2,1)S(1)} %pad_maximum_fusion.4), channel_id=1, source_target_pairs={{0,4},{1,5},{2,6},{3,7},{4,0},{5,1},{6,2},{7,3},{8,12},{9,13},{10,... | collective-permute-start | bytes 393224 | tf_op jit(solution)/shard_map/ppermute | solution.py:103
  200.8 5.3 %collective-permute-start.3 = (bf16[2,1,128,256]{3,2,1,0:T(8,128)(2,1)S(1)}, bf16[2,1,128,256]{3,2,1,0:T(8,128)(2,1)S(1)}, u32[]{:S(2)}, u32[]{:S(2)}) collective-permute-start(bf16[2,1,128,256]{3,2,1,0:T(8,128)(2,1)S(1)} %pad_maximum_fusion.5), channel_id=1, source_target_pairs={{0,8},{1,9},{2,10},{3,11},{4,12},{5,13},{6,14},{7,15},{8,0},{9,1},... | collective-permute-start | bytes 393224 | tf_op jit(solution)/shard_map/ppermute | solution.py:103
  208.7 12.0 %copy-start.8 = (bf16[3,256,256]{2,1,0:T(8,128)(2,1)S(1)}, bf16[3,256,256]{2,1,0:T(8,128)(2,1)}, u32[]{:S(2)}) copy-start(bf16[3,256,256]{2,1,0:T(8,128)(2,1)} %param.21) | copy-start | bytes 1179652
  209.0 6.6 %collective-permute-start.4 = (bf16[2,1,128,256]{3,2,1,0:T(8,128)(2,1)S(1)}, bf16[2,1,128,256]{3,2,1,0:T(8,128)(2,1)S(1)}, u32[]{:S(2)}, u32[]{:S(2)}) collective-permute-start(bf16[2,1,128,256]{3,2,1,0:T(8,128)(2,1)S(1)} %pad_maximum_fusion.6), channel_id=1, source_target_pairs={{0,16},{1,17},{2,18},{3,19},{4,20},{5,21},{6,22},{7,23},{8,24},{9,... | collective-permute-start | bytes 393224 | tf_op jit(solution)/shard_map/ppermute | solution.py:103
  217.4 5.8 %collective-permute-start.5 = (bf16[128,256]{1,0:T(8,128)(2,1)S(1)}, bf16[128,256]{1,0:T(8,128)(2,1)S(1)}, u32[]{:S(2)}, u32[]{:S(2)}) collective-permute-start(bf16[128,256]{1,0:T(8,128)(2,1)S(1)} %get-tuple-element.6), channel_id=1, source_target_pairs={{0,2},{1,3},{2,0},{3,1},{4,6},{5,7},{6,4},{7,5},{8,10},{9,11},{10,... | collective-permute-start | bytes 196616 | tf_op jit(solution)/shard_map/ppermute | solution.py:103
  223.3 6.6 %collective-permute-start.6 = (bf16[256,256]{1,0:T(8,128)(2,1)S(1)}, bf16[256,256]{1,0:T(8,128)(2,1)S(1)}, u32[]{:S(2)}, u32[]{:S(2)}) collective-permute-start(bf16[256,256]{1,0:T(8,128)(2,1)S(1)} %pad_maximum_fusion.7), channel_id=1, source_target_pairs={{0,16},{1,17},{2,18},{3,19},{4,20},{5,21},{6,22},{7,23},{8,24},{9,... | collective-permute-start | bytes 393224 | tf_op jit(solution)/shard_map/ppermute | solution.py:103
  229.9 6.5 %collective-permute-start.7 = (bf16[512,256]{1,0:T(8,128)(2,1)S(1)}, bf16[512,256]{1,0:T(8,128)(2,1)S(1)}, u32[]{:S(2)}, u32[]{:S(2)}) collective-permute-start(bf16[512,256]{1,0:T(8,128)(2,1)S(1)} %pad_maximum_fusion.1), channel_id=1, source_target_pairs={{0,1},{1,0},{2,3},{3,2},{4,5},{5,4},{6,7},{7,6},{8,9},{9,8},{10,11... | collective-permute-start | bytes 786440 | tf_op jit(solution)/shard_map/ppermute | solution.py:103
  236.4 9.3 %collective-permute-start.8 = (bf16[1024,256]{1,0:T(8,128)(2,1)S(1)}, bf16[1024,256]{1,0:T(8,128)(2,1)S(1)}, u32[]{:S(2)}, u32[]{:S(2)}) collective-permute-start(bf16[1024,256]{1,0:T(8,128)(2,1)S(1)} %pad_maximum_fusion), channel_id=1, source_target_pairs={{0,4},{1,5},{2,6},{3,7},{4,0},{5,1},{6,2},{7,3},{8,12},{9,13},{10,... | collective-permute-start | bytes 1572872 | tf_op jit(solution)/shard_map/ppermute | solution.py:103
  245.7 16.5 %collective-permute-start.9 = (bf16[2048,256]{1,0:T(8,128)(2,1)S(1)}, bf16[2048,256]{1,0:T(8,128)(2,1)S(1)}, u32[]{:S(2)}, u32[]{:S(2)}) collective-permute-start(bf16[2048,256]{1,0:T(8,128)(2,1)S(1)} %constant_dynamic-update-slice_fusion.8), channel_id=1, source_target_pairs={{0,8},{1,9},{2,10},{3,11},{4,12},{5,13},{6,14},{7,15},{8,0},{9,1},... | collective-permute-start | bytes 3145736 | tf_op jit(solution)/shard_map/ppermute | solution.py:103
  249.8 14.4 %copy-start.10 = (bf16[1,4096,1,1,1,1,256]{6,1,5,4,3,2,0:T(8,128)(2,1)S(1)}, bf16[1,4096,1,1,1,1,256]{6,1,5,4,3,2,0:T(8,128)(2,1)}, u32[]{:S(2)}) copy-start(bf16[1,4096,1,1,1,1,256]{6,1,5,4,3,2,0:T(8,128)(2,1)} %bitcast_dynamic-update-slice_fusion.3) | copy-start | bytes 6291460

commit v3 on v2

--- a/solution.py
+++ b/solution.py
@@ -33,6 +33,7 @@
     q = jnp.dot(normed, proj_ref[0], preferred_element_type=jnp.float32).astype(jnp.bfloat16)
     k = jnp.dot(normed, proj_ref[1], preferred_element_type=jnp.float32).astype(jnp.bfloat16)
     v = jnp.dot(normed, proj_ref[2], preferred_element_type=jnp.float32).astype(jnp.bfloat16)
+    k_t = k.T
     key_live = lax.broadcasted_iota(jnp.int32, (1, BALL), 1) < count
     lane = lax.broadcasted_iota(jnp.int32, (1, feature), 1)
     scale = 1.0 / math.sqrt(head_size)
@@ -41,7 +42,7 @@
         in_head = (lane >= h * head_size) & (lane < (h + 1) * head_size)
         qh = jnp.where(in_head, q, jnp.zeros((), jnp.bfloat16))
         vh = jnp.where(in_head, v, jnp.zeros((), jnp.bfloat16))
-        scores = lax.dot_general(qh, k, (((1,), (1,)), ((), ())), preferred_element_type=jnp.float32) * scale
+        scores = jnp.dot(qh, k_t, preferred_element_type=jnp.float32) * scale
         scores = jnp.where(key_live, scores, -1e30)
         row_max = jnp.max(scores, axis=-1, keepdims=True)
         expo = jnp.exp(scores - row_max)
@@ -76,19 +77,57 @@
     refined_ref[...] = fine.astype(jnp.float32) + jnp.dot(hidden, w2_ref[...], preferred_element_type=jnp.float32)
 
 
-def mlp_block(fine, mlp_in, mlp_out):
+def mlp_block(fine, refined, first_block, block_count, mlp_in, mlp_out):
     rows, feature = fine.shape
     ff = mlp_in.shape[1]
+    in_specs = [pl.BlockSpec((BALL, feature), lambda i: (first_block + i, 0)),
+                pl.BlockSpec((feature, ff), lambda i: (0, 0)),
+                pl.BlockSpec((ff, feature), lambda i: (0, 0))]
+    operands = [fine, mlp_in, mlp_out]
+    aliases = {}
+    if refined is not None:
+        in_specs.append(pl.BlockSpec(memory_space=pl.ANY))
+        operands.append(refined)
+        aliases = {3: 0}
+    kernel = _mlp_kernel if refined is None else (lambda f, w1, w2, _, out: _mlp_kernel(f, w1, w2, out))
     return pl.pallas_call(
-        _mlp_kernel,
+        kernel,
         out_shape=jax.ShapeDtypeStruct((rows, feature), jnp.float32),
-        grid=(rows // BALL,),
-        in_specs=[pl.BlockSpec((BALL, feature), lambda i: (i, 0)),
-                  pl.BlockSpec((feature, ff), lambda i: (0, 0)),
-                  pl.BlockSpec((ff, feature), lambda i: (0, 0))],
-        out_specs=pl.BlockSpec((BALL, feature), lambda i: (i, 0)),
+        grid=(block_count,),
+        in_specs=in_specs,
+        out_specs=pl.BlockSpec((BALL, feature), lambda i: (first_block + i, 0)),
+        input_output_aliases=aliases,
         compiler_params=pltpu.CompilerParams(dimension_semantics=("arbitrary",)),
-    )(fine, mlp_in, mlp_out)
+    )(*operands)
+
+
+def _final_kernel(counts_ref, refined_ref, unpooled_ref, out_ref):
+    slots, tokens, _ = unpooled_ref.shape
+    first_token = pl.program_id(0) * tokens
+    slot = lax.broadcasted_iota(jnp.int32, (slots, 1), 0)
+    for token in range(tokens):
+        ball = (first_token + token) * slots // BALL
+        start_in_ball = ((first_token + token) * slots) % BALL
+        live = start_in_ball + slot < counts_ref[ball]
+        rows = pl.ds(token * slots, slots)
+        total = refined_ref[rows, :] + unpooled_ref[:, token, :]
+        out_ref[rows, :] = jnp.where(live, total, 0.0).astype(out_ref.dtype)
+
+
+def final_block(ball_counts, refined, unpooled):
+    rows, feature = refined.shape
+    slots, tokens, _ = unpooled.shape
+    per_step = 8
+    return pl.pallas_call(
+        _final_kernel,
+        out_shape=jax.ShapeDtypeStruct((rows, feature), jnp.bfloat16),
+        grid_spec=pltpu.PrefetchScalarGridSpec(
+            num_scalar_prefetch=1, grid=(tokens // per_step,),
+            in_specs=[pl.BlockSpec((per_step * slots, feature), lambda i, c: (i, 0)),
+                      pl.BlockSpec((slots, per_step, feature), lambda i, c: (0, i, 0))],
+            out_specs=pl.BlockSpec((per_step * slots, feature), lambda i, c: (i, 0))),
+        compiler_params=pltpu.CompilerParams(dimension_semantics=("arbitrary",)),
+    )(ball_counts, refined, unpooled)
 
 
 def gather_all(shard, axis, order):
@@ -164,12 +203,13 @@
     live_mask = (jnp.arange(BALL, dtype=jnp.int32)[None, :] < ball_counts[:, None]).reshape(-1)
     masked = ball_block(tree_rows, ball_counts, ball_proj, ball_out)
     chunk = MLP_CHUNK_ROWS
-    refined_parts = []
+    refined = None
     for start in range(0, row_count, chunk):
-        refined_parts.append(mlp_block(masked[start:start + chunk], mlp_in, mlp_out))
-    pooled = jnp.dot(
-        masked.reshape(row_count // POOL, POOL * feature),
-        pool_weight,
+        refined = mlp_block(masked, refined, start // BALL, chunk // BALL, mlp_in, mlp_out)
+    pooled = jnp.einsum(
+        "rjd,jde->re",
+        masked.reshape(row_count // POOL, POOL, feature),
+        pool_weight.reshape(POOL, feature, feature),
         preferred_element_type=jnp.float32,
     )
     device_count = lax.axis_size("point")
@@ -195,11 +235,13 @@
     summary = (
         coarse_state + jnp.dot(mixed, global_out, preferred_element_type=jnp.float32)
     ).astype(jnp.bfloat16)
-    unpooled = jnp.dot(
-        summary.reshape(-1, feature), unpool_weight, preferred_element_type=jnp.float32
-    ).reshape(row_count, feature)
-    total = jnp.concatenate(refined_parts, axis=0) + unpooled
-    return jnp.where(live_mask[:, None], total, 0.0).astype(jnp.bfloat16)
+    unpooled = jnp.einsum(
+        "rd,dje->jre",
+        summary.reshape(-1, feature),
+        unpool_weight.reshape(feature, POOL, feature),
+        preferred_element_type=jnp.float32,
+    )
+    return final_block(ball_counts, refined, unpooled)
 
 
 def solution(mesh):

time: 317 us -> 292 us (0.921)
  local copies, waits for them, and re-layouts: 74 us -> 40.7 us
  Pallas kernels: 106 us -> 121 us
  other arithmetic: 20.8 us -> 10.7 us
  matrix products: 48.7 us -> 53 us
    reshape x2 -> x0, local copies, waits for them, and re-layouts: 16.6 us -> none  [the longest x1 9.28 us: local_body(): unpooled = jnp.dot(summary.reshape(-1, feature), unpool_weight, preferred...]
    pallas_call x8 -> x9, Pallas kernels: 43.1 us -> 57.6 us  [the longest x8 43 us: mlp_block(): pl.pallas_call(kernel, out_shape=jax.ShapeDtypeStruct((rows, feature), jn...]
    unnamed x42 -> x23, local copies, waits for them, and re-layouts: 15 us -> 3.62 us
    convert_element_type x1 -> x0, other arithmetic: 10.1 us -> none  [local_body(): return jnp.where(live_mask[:, None], total, 0.0).astype(jnp.bfloat16)]
    slice x1 -> x0, local copies, waits for them, and re-layouts: 4.25 us -> none  [local_body(): masked[start:start + chunk]]
    dot_general x2, matrix products: 14.1 us -> 17.7 us  [the longest x1 9.66 us: local_body(): jnp.einsum('rjd,jde->re', masked.reshape(row_count // POOL, POOL, feature...]
  transfers between devices with their start and end apart: 10 -> 10, of which waited for: 9 -> 9; matrix products, arithmetic and copies ran while one was open for 7% -> 2% of each run, Pallas kernels for 14% -> 15%
where the time goes in v3:
time: 292 us; the launch traced here: 290 us
  Pallas kernels  121 us (41%)
  matrix products  53 us (18%)
  waiting for transfers between devices  42.3 us (14%)
  local copies, waits for them, and re-layouts  40.7 us (14%)
  starting transfers between devices  22 us (8%)
  other arithmetic  10.7 us (4%)
    pallas_call x1, Pallas kernels, ball_block(): pl.pallas_call(_ball_kernel, out_shape=jax.ShapeDtypeStruct((rows, featur...  63.3 us
    pallas_call x8, Pallas kernels, mlp_block(): pl.pallas_call(kernel, out_shape=jax.ShapeDtypeStruct((rows, feature), jn...  43 us
    ppermute x10, waiting for transfers between devices, partner(): lax.ppermute(shard, axis, [(i, i ^ 1 << apart) for i in range(lax.axis_si...  42.3 us
    gather x1, local copies, waits for them, and re-layouts, local_body(): tree_rows = jnp.take(points, tree_order - offset, axis=0)  33.9 us
    ppermute x10, starting transfers between devices, partner(): lax.ppermute(shard, axis, [(i, i ^ 1 << apart) for i in range(lax.axis_si...  22 us
    pallas_call x1, Pallas kernels, final_block(): pl.pallas_call(_final_kernel, out_shape=jax.ShapeDtypeStruct((rows, featu...  14.7 us
    sub x6, matrix products, attend(): expo = jnp.exp(scores - row_max)  12.8 us
    dot_general x6, matrix products, attend(): jnp.einsum('bhqk,bkhd->bqhd', attn_probs, v_heads, preferred_element_type...  12.6 us
  transfers between devices with their start and end apart: 10, of which 9 were waited for; matrix products, arithmetic and copies ran while one was open for 2% of the time, Pallas kernels for 15%

profile of v3, /device:TPU:0, one launch (start us, length us, event | category | flops | bytes accessed | tf_op | source)
XLA Modules:
  0.0 290.3 jit_solution(6724334200901212892)
XLA Ops:
  0.0 0.8 fusion.133
  0.8 0.8 compare_and_fusion
  1.6 33.9 %gather_fusion = bf16[8192,256]{1,0:T(8,128)(2,1)} fusion(bf16[8192,256]{1,0:T(8,128)(2,1)} %param.13, s32[8192]{0:T(1024)S(1)} %fusion.133), kind=kCustom, calls=%fused_computation | custom fusion | bytes 8421376 | tf_op jit(solution)/shard_map/jit(_take)/gather | solution.py:202
  35.5 5.2 %broadcast_select_fusion.x_ref = bf16[8192,256]{1,0:T(8,128)(2,1)} fusion(bf16[8192,256]{1,0:T(8,128)(2,1)} %gather_fusion, pred[8192]{0:T(1024)(128)(4,1)S(1)} %compare_and_fusion), kind=kLoop, calls=%fused_computation.25 | loop fusion | flops 2097152 | bytes 8396800 | tf_op jit(solution)/shard_map/jit(_take)/select_n | solution.py:202
  40.7 63.3 %shard_map.127.fine_ref.f = bf16[8192,256]{1,0:T(8,128)(2,1)} custom-call(s32[32]{0:T(128)} %counts_ref.3, bf16[8192,256]{1,0:T(8,128)(2,1)} %broadcast_select_fusion.x_ref, bf16[3,256,256]{2,1,0:T(8,128)(2,1)} %proj_ref.1, bf16[256,256]{1,0:T(8,128)(2,1)} %wo_ref.1), custom_call_target="tpu_custom_call" | custom-call | tf_op jit(solution)/shard_map/pallas_call | solution.py:60
  104.1 9.7 %fusion.207 = (f32[128]{0:T(128)S(1)}, f32[128,256]{1,0:T(8,128)S(1)}) fusion(bf16[64,256,256]{2,1,0:T(8,128)(2,1)} %bitcast.271, bf16[128,64,256]{2,1,0:T(8,128)(2,1)} %bitcast.212), kind=kOutput, calls=%fused_computation.243 | convolution fusion | flops 1073774464 | bytes 12714496 | tf_op jit(solution)/shard_map/rjd,jde->re/dot_general | solution.py:209
  114.4 1.9 collective-permute-start
  116.9 5.4 %shard_map.128._ = f32[8192,256]{1,0:T(8,128)} custom-call(bf16[8192,256]{1,0:T(8,128)(2,1)} %shard_map.127.fine_ref.f, bf16[256,1024]{1,0:T(8,128)(2,1)} %w1.13, bf16[1024,256]{1,0:T(8,128)(2,1)} %w2.13), custom_call_target="tpu_custom_call" | custom-call | tf_op jit(solution)/shard_map/pallas_call | solution.py:93
  122.3 5.4 %shard_map.129._ = f32[8192,256]{1,0:T(8,128)} custom-call(bf16[8192,256]{1,0:T(8,128)(2,1)} %shard_map.127.fine_ref.f, bf16[256,1024]{1,0:T(8,128)(2,1)} %w1.13, bf16[1024,256]{1,0:T(8,128)(2,1)} %w2.13, f32[8192,256]{1,0:T(8,128)} %shard_map.128._), custom_call_target="tpu_custom_call", output_to_operand_aliasing={{}: (3, {})} | custom-call | tf_op jit(solution)/shard_map/pallas_call | solution.py:93
  127.7 5.4 %shard_map.130._ = f32[8192,256]{1,0:T(8,128)} custom-call(bf16[8192,256]{1,0:T(8,128)(2,1)} %shard_map.127.fine_ref.f, bf16[256,1024]{1,0:T(8,128)(2,1)} %w1.13, bf16[1024,256]{1,0:T(8,128)(2,1)} %w2.13, f32[8192,256]{1,0:T(8,128)} %shard_map.129._), custom_call_target="tpu_custom_call", output_to_operand_aliasing={{}: (3, {})} | custom-call | tf_op jit(solution)/shard_map/pallas_call | solution.py:93
  133.0 5.4 %shard_map.131._ = f32[8192,256]{1,0:T(8,128)} custom-call(bf16[8192,256]{1,0:T(8,128)(2,1)} %shard_map.127.fine_ref.f, bf16[256,1024]{1,0:T(8,128)(2,1)} %w1.13, bf16[1024,256]{1,0:T(8,128)(2,1)} %w2.13, f32[8192,256]{1,0:T(8,128)} %shard_map.130._), custom_call_target="tpu_custom_call", output_to_operand_aliasing={{}: (3, {})} | custom-call | tf_op jit(solution)/shard_map/pallas_call | solution.py:93
  138.4 5.4 %shard_map.132._ = f32[8192,256]{1,0:T(8,128)} custom-call(bf16[8192,256]{1,0:T(8,128)(2,1)} %shard_map.127.fine_ref.f, bf16[256,1024]{1,0:T(8,128)(2,1)} %w1.13, bf16[1024,256]{1,0:T(8,128)(2,1)} %w2.13, f32[8192,256]{1,0:T(8,128)} %shard_map.131._), custom_call_target="tpu_custom_call", output_to_operand_aliasing={{}: (3, {})} | custom-call | tf_op jit(solution)/shard_map/pallas_call | solution.py:93
  143.8 5.4 %shard_map.133._ = f32[8192,256]{1,0:T(8,128)} custom-call(bf16[8192,256]{1,0:T(8,128)(2,1)} %shard_map.127.fine_ref.f, bf16[256,1024]{1,0:T(8,128)(2,1)} %w1.13, bf16[1024,256]{1,0:T(8,128)(2,1)} %w2.13, f32[8192,256]{1,0:T(8,128)} %shard_map.132._), custom_call_target="tpu_custom_call", output_to_operand_aliasing={{}: (3, {})} | custom-call | tf_op jit(solution)/shard_map/pallas_call | solution.py:93
  149.1 5.4 %shard_map.134._ = f32[8192,256]{1,0:T(8,128)} custom-call(bf16[8192,256]{1,0:T(8,128)(2,1)} %shard_map.127.fine_ref.f, bf16[256,1024]{1,0:T(8,128)(2,1)} %w1.13, bf16[1024,256]{1,0:T(8,128)(2,1)} %w2.13, f32[8192,256]{1,0:T(8,128)} %shard_map.133._), custom_call_target="tpu_custom_call", output_to_operand_aliasing={{}: (3, {})} | custom-call | tf_op jit(solution)/shard_map/pallas_call | solution.py:93
  154.5 5.4 %shard_map.135.refined_ref = f32[8192,256]{1,0:T(8,128)} custom-call(bf16[8192,256]{1,0:T(8,128)(2,1)} %shard_map.127.fine_ref.f, bf16[256,1024]{1,0:T(8,128)(2,1)} %w1.13, bf16[1024,256]{1,0:T(8,128)(2,1)} %w2.13, f32[8192,256]{1,0:T(8,128)} %shard_map.134._), custom_call_target="tpu_custom_call", output_to_operand_aliasing={{}: (3, {})} | custom-call | tf_op jit(solution)/shard_map/pallas_call | solution.py:93
  160.2 0.7 fusion.208
  160.8 0.8 convolution_convert_fusion.6
  161.6 0.3 fusion.211
  161.9 0.2 multiply_reduce_fusion.5
  162.8 3.0 %collective-permute-start.1 = (bf16[2,1,128,256]{3,2,1,0:T(8,128)(2,1)S(1)}, bf16[2,1,128,256]{3,2,1,0:T(8,128)(2,1)S(1)}, u32[]{:S(2)}, u32[]{:S(2)}) collective-permute-start(bf16[2,1,128,256]{3,2,1,0:T(8,128)(2,1)S(1)} %pad_maximum_fusion.3), channel_id=1, source_target_pairs={{0,2},{1,3},{2,0},{3,1},{4,6},{5,7},{6,4},{7,5},{8,10},{9,11},{10,... | collective-permute-start | bytes 393224 | tf_op jit(solution)/shard_map/ppermute | solution.py:142
  166.1 3.3 %collective-permute-done.1 = bf16[2,1,128,256]{3,2,1,0:T(8,128)(2,1)S(1)} collective-permute-done((bf16[2,1,128,256]{3,2,1,0:T(8,128)(2,1)S(1)}, bf16[2,1,128,256]{3,2,1,0:T(8,128)(2,1)S(1)}, u32[]{:S(2)}, u32[]{:S(2)}) %collective-permute-start.1) | collective-permute-done | bytes 131104 | tf_op jit(solution)/shard_map/ppermute | solution.py:142
  169.6 0.7 fusion.212
  170.3 0.8 convolution_convert_fusion.5
  171.0 0.3 fusion.215
  172.3 2.0 collective-permute-start.2
  174.6 2.7 collective-permute-done.2
  177.6 0.7 fusion.216
  178.2 0.8 convolution_convert_fusion.4
  179.0 0.3 fusion.219
  180.2 1.8 collective-permute-start.3
  182.3 3.2 %collective-permute-done.3 = bf16[2,1,128,256]{3,2,1,0:T(8,128)(2,1)S(1)} collective-permute-done((bf16[2,1,128,256]{3,2,1,0:T(8,128)(2,1)S(1)}, bf16[2,1,128,256]{3,2,1,0:T(8,128)(2,1)S(1)}, u32[]{:S(2)}, u32[]{:S(2)}) %collective-permute-start.3) | collective-permute-done | bytes 131104 | tf_op jit(solution)/shard_map/ppermute | solution.py:142
  185.8 0.6 fusion.220
  186.4 0.8 convolution_convert_fusion.3
  187.2 0.3 fusion.223
  187.5 0.2 multiply_reduce_fusion.2
  188.4 3.1 %collective-permute-start.4 = (bf16[2,1,128,256]{3,2,1,0:T(8,128)(2,1)S(1)}, bf16[2,1,128,256]{3,2,1,0:T(8,128)(2,1)S(1)}, u32[]{:S(2)}, u32[]{:S(2)}) collective-permute-start(bf16[2,1,128,256]{3,2,1,0:T(8,128)(2,1)S(1)} %pad_maximum_fusion.6), channel_id=1, source_target_pairs={{0,16},{1,17},{2,18},{3,19},{4,20},{5,21},{6,22},{7,23},{8,24},{9,... | collective-permute-start | bytes 393224 | tf_op jit(solution)/shard_map/ppermute | solution.py:142
  191.8 3.2 %collective-permute-done.4 = bf16[2,1,128,256]{3,2,1,0:T(8,128)(2,1)S(1)} collective-permute-done((bf16[2,1,128,256]{3,2,1,0:T(8,128)(2,1)S(1)}, bf16[2,1,128,256]{3,2,1,0:T(8,128)(2,1)S(1)}, u32[]{:S(2)}, u32[]{:S(2)}) %collective-permute-start.4) | collective-permute-done | bytes 131104 | tf_op jit(solution)/shard_map/ppermute | solution.py:142
  195.2 0.7 fusion.224
  195.9 0.8 convolution_convert_fusion.2
  196.7 0.2 bitcast_dynamic-update-slice_fusion.9
  196.9 3.0 %collective-permute-start.5 = (bf16[128,256]{1,0:T(8,128)(2,1)S(1)}, bf16[128,256]{1,0:T(8,128)(2,1)S(1)}, u32[]{:S(2)}, u32[]{:S(2)}) collective-permute-start(bf16[128,256]{1,0:T(8,128)(2,1)S(1)} %get-tuple-element.6), channel_id=1, source_target_pairs={{0,2},{1,3},{2,0},{3,1},{4,6},{5,7},{6,4},{7,5},{8,10},{9,11},{10,... | collective-permute-start | bytes 196616 | tf_op jit(solution)/shard_map/ppermute | solution.py:142
  200.2 0.2 convolution_convert_fusion.7
  200.4 2.3 collective-permute-done.5
  202.7 3.1 %collective-permute-start.6 = (bf16[256,256]{1,0:T(8,128)(2,1)S(1)}, bf16[256,256]{1,0:T(8,128)(2,1)S(1)}, u32[]{:S(2)}, u32[]{:S(2)}) collective-permute-start(bf16[256,256]{1,0:T(8,128)(2,1)S(1)} %pad_maximum_fusion.7), channel_id=1, source_target_pairs={{0,16},{1,17},{2,18},{3,19},{4,20},{5,21},{6,22},{7,23},{8,24},{9,... | collective-permute-start | bytes 393224 | tf_op jit(solution)/shard_map/ppermute | solution.py:142
  205.8 0.6 bitcast_dynamic-update-slice_fusion.11
  206.6 2.7 collective-permute-done.6
  209.3 0.4 collective-permute-start.7
  209.7 0.6 bitcast_dynamic-update-slice_fusion.10
  210.4 5.4 %collective-permute-done.7 = bf16[512,256]{1,0:T(8,128)(2,1)S(1)} collective-permute-done((bf16[512,256]{1,0:T(8,128)(2,1)S(1)}, bf16[512,256]{1,0:T(8,128)(2,1)S(1)}, u32[]{:S(2)}, u32[]{:S(2)}) %collective-permute-start.7) | collective-permute-done | bytes 262176 | tf_op jit(solution)/shard_map/ppermute | solution.py:142
  215.8 2.0 collective-permute-start.8
  217.9 7.2 %collective-permute-done.8 = bf16[1024,256]{1,0:T(8,128)(2,1)S(1)} collective-permute-done((bf16[1024,256]{1,0:T(8,128)(2,1)S(1)}, bf16[1024,256]{1,0:T(8,128)(2,1)S(1)}, u32[]{:S(2)}, u32[]{:S(2)}) %collective-permute-start.8) | collective-permute-done | bytes 524320 | tf_op jit(solution)/shard_map/ppermute | solution.py:142
  225.1 1.6 collective-permute-start.9
  226.7 0.7 bitcast_dynamic-update-slice_fusion.7
  227.4 0.7 bitcast_dynamic-update-slice_fusion.5
  228.1 0.8 bitcast_dynamic-update-slice_fusion.3
  229.0 12.4 %collective-permute-done.9 = bf16[2048,256]{1,0:T(8,128)(2,1)S(1)} collective-permute-done((bf16[2048,256]{1,0:T(8,128)(2,1)S(1)}, bf16[2048,256]{1,0:T(8,128)(2,1)S(1)}, u32[]{:S(2)}, u32[]{:S(2)}) %collective-permute-start.9) | collective-permute-done | bytes 1048608 | tf_op jit(solution)/shard_map/ppermute | solution.py:142
  241.4 0.6 convert_reduce_fusion
  242.1 1.3 fusion.15
  243.5 3.9 %convolution_convert_fusion = bf16[4096,256]{0,1:T(8,128)(2,1)} fusion(bf16[3,256,256]{2,1,0:T(8,128)(2,1)S(1)} %copy-done.3, bf16[1,4096,1,1,1,1,256]{6,1,5,4,3,2,0:T(8,128)(2,1)S(1)} %bitcast_dynamic-update-slice_fusion.1, f32[4096]{0:T(1024)S(1)} %add_rsqrt_fusion, f32[4096]{0:T(1024)S(1)} %broadcast_multiply_fusion), kind=kOutput, calls=%fused_computation.18 | convolution fusion | flops 542113792 | bytes 4358144 | tf_op jit(solution)/shard_map/dot_general | solution.py:153
  247.4 1.9 convolution_convert_fusion.1
  249.3 9.6 %fusion.227 = (f32[8,128]{1,0:T(8,128)S(1)}, f32[8,128,4096]{2,1,0:T(8,128)}) fusion(bf16[128,8,32]{0,2,1:T(8,128)(2,1)S(1)} %bitcast.226, bf16[4096,8,32]{0,2,1:T(8,128)(2,1)} %bitcast.273), kind=kOutput, calls=%fused_computation.253 | convolution fusion | flops 281022464 | bytes 18944000 | tf_op jit(solution)/shard_map/sub | solution.py:169
  258.9 8.8 %fusion.37 = bf16[8,32,128]{2,1,0:T(8,128)(2,1)S(1)} fusion(bf16[4096,8,32]{0,2,1:T(8,128)(2,1)S(1)} %bitcast.272, f32[8,128,4096]{2,1,0:T(8,128)} %get-tuple-element.29, f32[8,128]{1,0:T(8,128)S(1)} %get-tuple-element.28), kind=kOutput, calls=%fused_computation.51 | convolution fusion | flops 276856832 | bytes 18944000 | tf_op jit(solution)/shard_map/bhqk,bkhd->bqhd/dot_general | solution.py:171
  267.6 8.1 %fusion.18.unpooled_ref = f32[64,128,256]{2,1,0:T(8,128)} fusion(bf16[32,64,8,256]{3,2,1,0:T(8,128)(2,1)} %bitcast.213, f32[128,256]{1,0:T(8,128)S(1)} %get-tuple-element.27, bf16[128,256]{0,1:T(8,128)(2,1)S(1)} %bitcast.224, bf16[256,256]{1,0:T(8,128)(2,1)S(1)} %copy-done), kind=kOutput, calls=%fused_computation.26 | convolution fusion | flops 1090584576 | bytes 17104896 | tf_op jit(solution)/shard_map/rd,dje->jre/dot_general | solution.py:238
  275.7 14.7 %shard_map.136 = bf16[8192,256]{1,0:T(8,128)(2,1)} custom-call(s32[32]{0:T(128)} %counts_ref.3, f32[8192,256]{1,0:T(8,128)} %shard_map.135.refined_ref, f32[64,128,256]{2,1,0:T(8,128)} %fusion.18.unpooled_ref), custom_call_target="tpu_custom_call" | custom-call | tf_op jit(solution)/shard_map/pallas_call | solution.py:121
  (100 shorter events, 7.3 us)
Async XLA Ops:
  0.0 267.6 %copy-start = (bf16[256,256]{1,0:T(8,128)(2,1)S(1)}, bf16[256,256]{1,0:T(8,128)(2,1)}, u32[]{:S(2)}) copy-start(bf16[256,256]{1,0:T(8,128)(2,1)} %param.22) | copy-start | bytes 393220
  104.1 10.0 %copy-start.1 = (bf16[3,256,256]{2,1,0:T(8,128)(2,1)S(1)}, bf16[3,256,256]{2,1,0:T(8,128)(2,1)}, u32[]{:S(2)}) copy-start(bf16[3,256,256]{2,1,0:T(8,128)(2,1)} %param.19) | copy-start | bytes 1179652
  114.4 45.5 %collective-permute-start = (bf16[2,1,128,256]{3,2,1,0:T(8,128)(2,1)S(1)}, bf16[2,1,128,256]{3,2,1,0:T(8,128)(2,1)S(1)}, u32[]{:S(2)}, u32[]{:S(2)}) collective-permute-start(bf16[2,1,128,256]{3,2,1,0:T(8,128)(2,1)S(1)} %pad_maximum_fusion.2), channel_id=1, source_target_pairs={{0,1},{1,0},{2,3},{3,2},{4,5},{5,4},{6,7},{7,6},{8,9},{9,8},{10,11... | collective-permute-start | bytes 393224 | tf_op jit(solution)/shard_map/ppermute | solution.py:142
  159.9 1.7 copy-start.2
  162.8 6.6 %collective-permute-start.1 = (bf16[2,1,128,256]{3,2,1,0:T(8,128)(2,1)S(1)}, bf16[2,1,128,256]{3,2,1,0:T(8,128)(2,1)S(1)}, u32[]{:S(2)}, u32[]{:S(2)}) collective-permute-start(bf16[2,1,128,256]{3,2,1,0:T(8,128)(2,1)S(1)} %pad_maximum_fusion.3), channel_id=1, source_target_pairs={{0,2},{1,3},{2,0},{3,1},{4,6},{5,7},{6,4},{7,5},{8,10},{9,11},{10,... | collective-permute-start | bytes 393224 | tf_op jit(solution)/shard_map/ppermute | solution.py:142
  172.3 5.0 %collective-permute-start.2 = (bf16[2,1,128,256]{3,2,1,0:T(8,128)(2,1)S(1)}, bf16[2,1,128,256]{3,2,1,0:T(8,128)(2,1)S(1)}, u32[]{:S(2)}, u32[]{:S(2)}) collective-permute-start(bf16[2,1,128,256]{3,2,1,0:T(8,128)(2,1)S(1)} %pad_maximum_fusion.4), channel_id=1, source_target_pairs={{0,4},{1,5},{2,6},{3,7},{4,0},{5,1},{6,2},{7,3},{8,12},{9,13},{10,... | collective-permute-start | bytes 393224 | tf_op jit(solution)/shard_map/ppermute | solution.py:142
  180.2 5.3 %collective-permute-start.3 = (bf16[2,1,128,256]{3,2,1,0:T(8,128)(2,1)S(1)}, bf16[2,1,128,256]{3,2,1,0:T(8,128)(2,1)S(1)}, u32[]{:S(2)}, u32[]{:S(2)}) collective-permute-start(bf16[2,1,128,256]{3,2,1,0:T(8,128)(2,1)S(1)} %pad_maximum_fusion.5), channel_id=1, source_target_pairs={{0,8},{1,9},{2,10},{3,11},{4,12},{5,13},{6,14},{7,15},{8,0},{9,1},... | collective-permute-start | bytes 393224 | tf_op jit(solution)/shard_map/ppermute | solution.py:142
  188.2 12.0 %copy-start.3 = (bf16[3,256,256]{2,1,0:T(8,128)(2,1)S(1)}, bf16[3,256,256]{2,1,0:T(8,128)(2,1)}, u32[]{:S(2)}) copy-start(bf16[3,256,256]{2,1,0:T(8,128)(2,1)} %param.21) | copy-start | bytes 1179652
  188.4 6.6 %collective-permute-start.4 = (bf16[2,1,128,256]{3,2,1,0:T(8,128)(2,1)S(1)}, bf16[2,1,128,256]{3,2,1,0:T(8,128)(2,1)S(1)}, u32[]{:S(2)}, u32[]{:S(2)}) collective-permute-start(bf16[2,1,128,256]{3,2,1,0:T(8,128)(2,1)S(1)} %pad_maximum_fusion.6), channel_id=1, source_target_pairs={{0,16},{1,17},{2,18},{3,19},{4,20},{5,21},{6,22},{7,23},{8,24},{9,... | collective-permute-start | bytes 393224 | tf_op jit(solution)/shard_map/ppermute | solution.py:142
  196.9 5.8 %collective-permute-start.5 = (bf16[128,256]{1,0:T(8,128)(2,1)S(1)}, bf16[128,256]{1,0:T(8,128)(2,1)S(1)}, u32[]{:S(2)}, u32[]{:S(2)}) collective-permute-start(bf16[128,256]{1,0:T(8,128)(2,1)S(1)} %get-tuple-element.6), channel_id=1, source_target_pairs={{0,2},{1,3},{2,0},{3,1},{4,6},{5,7},{6,4},{7,5},{8,10},{9,11},{10,... | collective-permute-start | bytes 196616 | tf_op jit(solution)/shard_map/ppermute | solution.py:142
  202.7 6.6 %collective-permute-start.6 = (bf16[256,256]{1,0:T(8,128)(2,1)S(1)}, bf16[256,256]{1,0:T(8,128)(2,1)S(1)}, u32[]{:S(2)}, u32[]{:S(2)}) collective-permute-start(bf16[256,256]{1,0:T(8,128)(2,1)S(1)} %pad_maximum_fusion.7), channel_id=1, source_target_pairs={{0,16},{1,17},{2,18},{3,19},{4,20},{5,21},{6,22},{7,23},{8,24},{9,... | collective-permute-start | bytes 393224 | tf_op jit(solution)/shard_map/ppermute | solution.py:142
  209.3 6.5 %collective-permute-start.7 = (bf16[512,256]{1,0:T(8,128)(2,1)S(1)}, bf16[512,256]{1,0:T(8,128)(2,1)S(1)}, u32[]{:S(2)}, u32[]{:S(2)}) collective-permute-start(bf16[512,256]{1,0:T(8,128)(2,1)S(1)} %pad_maximum_fusion.1), channel_id=1, source_target_pairs={{0,1},{1,0},{2,3},{3,2},{4,5},{5,4},{6,7},{7,6},{8,9},{9,8},{10,11... | collective-permute-start | bytes 786440 | tf_op jit(solution)/shard_map/ppermute | solution.py:142
  215.8 9.3 %collective-permute-start.8 = (bf16[1024,256]{1,0:T(8,128)(2,1)S(1)}, bf16[1024,256]{1,0:T(8,128)(2,1)S(1)}, u32[]{:S(2)}, u32[]{:S(2)}) collective-permute-start(bf16[1024,256]{1,0:T(8,128)(2,1)S(1)} %pad_maximum_fusion), channel_id=1, source_target_pairs={{0,4},{1,5},{2,6},{3,7},{4,0},{5,1},{6,2},{7,3},{8,12},{9,13},{10,... | collective-permute-start | bytes 1572872 | tf_op jit(solution)/shard_map/ppermute | solution.py:142
  225.1 16.3 %collective-permute-start.9 = (bf16[2048,256]{1,0:T(8,128)(2,1)S(1)}, bf16[2048,256]{1,0:T(8,128)(2,1)S(1)}, u32[]{:S(2)}, u32[]{:S(2)}) collective-permute-start(bf16[2048,256]{1,0:T(8,128)(2,1)S(1)} %constant_dynamic-update-slice_fusion), channel_id=1, source_target_pairs={{0,8},{1,9},{2,10},{3,11},{4,12},{5,13},{6,14},{7,15},{8,0},{9,1},... | collective-permute-start | bytes 3145736 | tf_op jit(solution)/shard_map/ppermute | solution.py:142
  229.0 14.4 %copy-start.4 = (bf16[1,4096,1,1,1,1,256]{6,1,5,4,3,2,0:T(8,128)(2,1)S(1)}, bf16[1,4096,1,1,1,1,256]{6,1,5,4,3,2,0:T(8,128)(2,1)}, u32[]{:S(2)}) copy-start(bf16[1,4096,1,1,1,1,256]{6,1,5,4,3,2,0:T(8,128)(2,1)} %bitcast_dynamic-update-slice_fusion.3) | copy-start | bytes 6291460

commit v4 on v3

--- a/solution.py
+++ b/solution.py
@@ -101,16 +101,34 @@
     )(*operands)
 
 
-def _final_kernel(counts_ref, refined_ref, unpooled_ref, out_ref):
-    slots, tokens, _ = unpooled_ref.shape
-    first_token = pl.program_id(0) * tokens
+def _final_kernel(counts_ref, refined_ref, unpooled_hbm, out_ref, staged, arrived):
+    step = pl.program_id(0)
+    tokens, slots, _ = staged.shape[1:]
+
+    def fetch(at, into):
+        for token in range(tokens):
+            pltpu.make_async_copy(
+                unpooled_hbm.at[:, at * tokens + token, :], staged.at[into, token], arrived.at[into]
+            ).start()
+
+    @pl.when(step == 0)
+    def _():
+        fetch(0, 0)
+
+    @pl.when(step + 1 < pl.num_programs(0))
+    def _():
+        fetch(step + 1, (step + 1) % 2)
+
+    current = step % 2
+    pltpu.make_async_copy(
+        unpooled_hbm.at[pl.ds(0, tokens), pl.ds(0, slots), :], staged.at[current], arrived.at[current]
+    ).wait()
     slot = lax.broadcasted_iota(jnp.int32, (slots, 1), 0)
     for token in range(tokens):
-        ball = (first_token + token) * slots // BALL
-        start_in_ball = ((first_token + token) * slots) % BALL
-        live = start_in_ball + slot < counts_ref[ball]
+        first_row = (step * tokens + token) * slots
+        live = first_row % BALL + slot < counts_ref[first_row // BALL]
         rows = pl.ds(token * slots, slots)
-        total = refined_ref[rows, :] + unpooled_ref[:, token, :]
+        total = refined_ref[rows, :] + staged[current, token]
         out_ref[rows, :] = jnp.where(live, total, 0.0).astype(out_ref.dtype)
 
 
@@ -124,8 +142,10 @@
         grid_spec=pltpu.PrefetchScalarGridSpec(
             num_scalar_prefetch=1, grid=(tokens // per_step,),
             in_specs=[pl.BlockSpec((per_step * slots, feature), lambda i, c: (i, 0)),
-                      pl.BlockSpec((slots, per_step, feature), lambda i, c: (0, i, 0))],
-            out_specs=pl.BlockSpec((per_step * slots, feature), lambda i, c: (i, 0))),
+                      pl.BlockSpec(memory_space=pl.ANY)],
+            out_specs=pl.BlockSpec((per_step * slots, feature), lambda i, c: (i, 0)),
+            scratch_shapes=[pltpu.VMEM((2, per_step, slots, feature), jnp.float32),
+                            pltpu.SemaphoreType.DMA((2,))]),
         compiler_params=pltpu.CompilerParams(dimension_semantics=("arbitrary",)),
     )(ball_counts, refined, unpooled)
 
@@ -199,7 +219,7 @@
 ):
     row_count, feature = points.shape
     offset = lax.axis_index("point") * row_count
-    tree_rows = jnp.take(points, tree_order - offset, axis=0)
+    tree_rows = points.at[tree_order - offset].get(mode="promise_in_bounds", unique_indices=True)
     live_mask = (jnp.arange(BALL, dtype=jnp.int32)[None, :] < ball_counts[:, None]).reshape(-1)
     masked = ball_block(tree_rows, ball_counts, ball_proj, ball_out)
     chunk = MLP_CHUNK_ROWS

time: 292 us -> 287 us (0.983)
  other arithmetic: 10.7 us -> 4.67 us
    select_n x1 -> x0, other arithmetic: 5.23 us -> none  [local_body(): tree_rows = jnp.take(points, tree_order - offset, axis=0)]
where the time goes in v4:
time: 287 us; the launch traced here: 286 us
  Pallas kernels  122 us (43%)
  matrix products  53 us (18%)
  waiting for transfers between devices  42.3 us (15%)
  local copies, waits for them, and re-layouts  40.7 us (14%)
  starting transfers between devices  22 us (8%)
  other arithmetic  4.67 us (2%)
    pallas_call x1, Pallas kernels, ball_block(): pl.pallas_call(_ball_kernel, out_shape=jax.ShapeDtypeStruct((rows, featur...  63.3 us
    pallas_call x8, Pallas kernels, mlp_block(): pl.pallas_call(kernel, out_shape=jax.ShapeDtypeStruct((rows, feature), jn...  43 us
    ppermute x10, waiting for transfers between devices, partner(): lax.ppermute(shard, axis, [(i, i ^ 1 << apart) for i in range(lax.axis_si...  42.3 us
    gather x1, local copies, waits for them, and re-layouts, local_body(): points.at[tree_order - offset]  33.9 us
    ppermute x10, starting transfers between devices, partner(): lax.ppermute(shard, axis, [(i, i ^ 1 << apart) for i in range(lax.axis_si...  22 us
    pallas_call x1, Pallas kernels, final_block(): pl.pallas_call(_final_kernel, out_shape=jax.ShapeDtypeStruct((rows, featu...  15.7 us
    sub x6, matrix products, attend(): expo = jnp.exp(scores - row_max)  12.8 us
    dot_general x6, matrix products, attend(): jnp.einsum('bhqk,bkhd->bqhd', attn_probs, v_heads, preferred_element_type...  12.6 us
  transfers between devices with their start and end apart: 10, of which 9 were waited for; matrix products, arithmetic and copies ran while one was open for 2% of the time, Pallas kernels for 15%

profile of v4, /device:TPU:0, one launch (start us, length us, event | category | flops | bytes accessed | tf_op | source)
XLA Modules:
  0.0 285.6 jit_solution(13048688577529430849)
XLA Ops:
  0.0 0.8 fusion.133
  0.8 33.9 %gather_fusion = bf16[8192,256]{1,0:T(8,128)(2,1)} fusion(bf16[8192,256]{1,0:T(8,128)(2,1)} %param.13, s32[8192]{0:T(1024)S(1)} %fusion.133), kind=kCustom, calls=%fused_computation | custom fusion | bytes 8421376 | tf_op jit(solution)/shard_map/gather | solution.py:222
  34.7 63.3 %shard_map.127.fine_ref.f = bf16[8192,256]{1,0:T(8,128)(2,1)} custom-call(s32[32]{0:T(128)} %counts_ref.3, bf16[8192,256]{1,0:T(8,128)(2,1)} %gather_fusion, bf16[3,256,256]{2,1,0:T(8,128)(2,1)} %proj_ref.1, bf16[256,256]{1,0:T(8,128)(2,1)} %wo_ref.1), custom_call_target="tpu_custom_call" | custom-call | tf_op jit(solution)/shard_map/pallas_call | solution.py:60
  98.0 9.7 %fusion.207 = (f32[128]{0:T(128)S(1)}, f32[128,256]{1,0:T(8,128)S(1)}) fusion(bf16[64,256,256]{2,1,0:T(8,128)(2,1)} %bitcast.271, bf16[128,64,256]{2,1,0:T(8,128)(2,1)} %bitcast.212), kind=kOutput, calls=%fused_computation.241 | convolution fusion | flops 1073774464 | bytes 12714496 | tf_op jit(solution)/shard_map/rjd,jde->re/dot_general | solution.py:229
  108.4 1.9 collective-permute-start
  110.9 5.4 %shard_map.128._ = f32[8192,256]{1,0:T(8,128)} custom-call(bf16[8192,256]{1,0:T(8,128)(2,1)} %shard_map.127.fine_ref.f, bf16[256,1024]{1,0:T(8,128)(2,1)} %w1.13, bf16[1024,256]{1,0:T(8,128)(2,1)} %w2.13), custom_call_target="tpu_custom_call" | custom-call | tf_op jit(solution)/shard_map/pallas_call | solution.py:93
  116.3 5.4 %shard_map.129._ = f32[8192,256]{1,0:T(8,128)} custom-call(bf16[8192,256]{1,0:T(8,128)(2,1)} %shard_map.127.fine_ref.f, bf16[256,1024]{1,0:T(8,128)(2,1)} %w1.13, bf16[1024,256]{1,0:T(8,128)(2,1)} %w2.13, f32[8192,256]{1,0:T(8,128)} %shard_map.128._), custom_call_target="tpu_custom_call", output_to_operand_aliasing={{}: (3, {})} | custom-call | tf_op jit(solution)/shard_map/pallas_call | solution.py:93
  121.6 5.4 %shard_map.130._ = f32[8192,256]{1,0:T(8,128)} custom-call(bf16[8192,256]{1,0:T(8,128)(2,1)} %shard_map.127.fine_ref.f, bf16[256,1024]{1,0:T(8,128)(2,1)} %w1.13, bf16[1024,256]{1,0:T(8,128)(2,1)} %w2.13, f32[8192,256]{1,0:T(8,128)} %shard_map.129._), custom_call_target="tpu_custom_call", output_to_operand_aliasing={{}: (3, {})} | custom-call | tf_op jit(solution)/shard_map/pallas_call | solution.py:93
  127.0 5.4 %shard_map.131._ = f32[8192,256]{1,0:T(8,128)} custom-call(bf16[8192,256]{1,0:T(8,128)(2,1)} %shard_map.127.fine_ref.f, bf16[256,1024]{1,0:T(8,128)(2,1)} %w1.13, bf16[1024,256]{1,0:T(8,128)(2,1)} %w2.13, f32[8192,256]{1,0:T(8,128)} %shard_map.130._), custom_call_target="tpu_custom_call", output_to_operand_aliasing={{}: (3, {})} | custom-call | tf_op jit(solution)/shard_map/pallas_call | solution.py:93
  132.4 5.4 %shard_map.132._ = f32[8192,256]{1,0:T(8,128)} custom-call(bf16[8192,256]{1,0:T(8,128)(2,1)} %shard_map.127.fine_ref.f, bf16[256,1024]{1,0:T(8,128)(2,1)} %w1.13, bf16[1024,256]{1,0:T(8,128)(2,1)} %w2.13, f32[8192,256]{1,0:T(8,128)} %shard_map.131._), custom_call_target="tpu_custom_call", output_to_operand_aliasing={{}: (3, {})} | custom-call | tf_op jit(solution)/shard_map/pallas_call | solution.py:93
  137.8 5.4 %shard_map.133._ = f32[8192,256]{1,0:T(8,128)} custom-call(bf16[8192,256]{1,0:T(8,128)(2,1)} %shard_map.127.fine_ref.f, bf16[256,1024]{1,0:T(8,128)(2,1)} %w1.13, bf16[1024,256]{1,0:T(8,128)(2,1)} %w2.13, f32[8192,256]{1,0:T(8,128)} %shard_map.132._), custom_call_target="tpu_custom_call", output_to_operand_aliasing={{}: (3, {})} | custom-call | tf_op jit(solution)/shard_map/pallas_call | solution.py:93
  143.1 5.4 %shard_map.134._ = f32[8192,256]{1,0:T(8,128)} custom-call(bf16[8192,256]{1,0:T(8,128)(2,1)} %shard_map.127.fine_ref.f, bf16[256,1024]{1,0:T(8,128)(2,1)} %w1.13, bf16[1024,256]{1,0:T(8,128)(2,1)} %w2.13, f32[8192,256]{1,0:T(8,128)} %shard_map.133._), custom_call_target="tpu_custom_call", output_to_operand_aliasing={{}: (3, {})} | custom-call | tf_op jit(solution)/shard_map/pallas_call | solution.py:93
  148.5 5.4 %shard_map.135.refined_ref = f32[8192,256]{1,0:T(8,128)} custom-call(bf16[8192,256]{1,0:T(8,128)(2,1)} %shard_map.127.fine_ref.f, bf16[256,1024]{1,0:T(8,128)(2,1)} %w1.13, bf16[1024,256]{1,0:T(8,128)(2,1)} %w2.13, f32[8192,256]{1,0:T(8,128)} %shard_map.134._), custom_call_target="tpu_custom_call", output_to_operand_aliasing={{}: (3, {})} | custom-call | tf_op jit(solution)/shard_map/pallas_call | solution.py:93
  154.1 0.7 fusion.208
  154.8 0.8 convolution_convert_fusion.6
  155.6 0.3 fusion.211
  155.9 0.2 multiply_reduce_fusion.5
  156.8 3.0 %collective-permute-start.1 = (bf16[2,1,128,256]{3,2,1,0:T(8,128)(2,1)S(1)}, bf16[2,1,128,256]{3,2,1,0:T(8,128)(2,1)S(1)}, u32[]{:S(2)}, u32[]{:S(2)}) collective-permute-start(bf16[2,1,128,256]{3,2,1,0:T(8,128)(2,1)S(1)} %pad_maximum_fusion.3), channel_id=1, source_target_pairs={{0,2},{1,3},{2,0},{3,1},{4,6},{5,7},{6,4},{7,5},{8,10},{9,11},{10,... | collective-permute-start | bytes 393224 | tf_op jit(solution)/shard_map/ppermute | solution.py:162
  160.1 3.3 %collective-permute-done.1 = bf16[2,1,128,256]{3,2,1,0:T(8,128)(2,1)S(1)} collective-permute-done((bf16[2,1,128,256]{3,2,1,0:T(8,128)(2,1)S(1)}, bf16[2,1,128,256]{3,2,1,0:T(8,128)(2,1)S(1)}, u32[]{:S(2)}, u32[]{:S(2)}) %collective-permute-start.1) | collective-permute-done | bytes 131104 | tf_op jit(solution)/shard_map/ppermute | solution.py:162
  163.6 0.7 fusion.212
  164.3 0.8 convolution_convert_fusion.5
  165.0 0.3 fusion.215
  165.3 0.2 multiply_reduce_fusion.4
  166.3 2.0 collective-permute-start.2
  168.6 2.7 collective-permute-done.2
  171.6 0.7 fusion.216
  172.2 0.8 convolution_convert_fusion.4
  173.0 0.3 fusion.219
  173.3 0.2 multiply_reduce_fusion.3
  174.2 1.8 collective-permute-start.3
  176.3 3.2 %collective-permute-done.3 = bf16[2,1,128,256]{3,2,1,0:T(8,128)(2,1)S(1)} collective-permute-done((bf16[2,1,128,256]{3,2,1,0:T(8,128)(2,1)S(1)}, bf16[2,1,128,256]{3,2,1,0:T(8,128)(2,1)S(1)}, u32[]{:S(2)}, u32[]{:S(2)}) %collective-permute-start.3) | collective-permute-done | bytes 131104 | tf_op jit(solution)/shard_map/ppermute | solution.py:162
  179.7 0.6 fusion.220
  180.4 0.8 convolution_convert_fusion.3
  181.2 0.3 fusion.223
  181.5 0.2 multiply_reduce_fusion.2
  182.4 3.1 %collective-permute-start.4 = (bf16[2,1,128,256]{3,2,1,0:T(8,128)(2,1)S(1)}, bf16[2,1,128,256]{3,2,1,0:T(8,128)(2,1)S(1)}, u32[]{:S(2)}, u32[]{:S(2)}) collective-permute-start(bf16[2,1,128,256]{3,2,1,0:T(8,128)(2,1)S(1)} %pad_maximum_fusion.6), channel_id=1, source_target_pairs={{0,16},{1,17},{2,18},{3,19},{4,20},{5,21},{6,22},{7,23},{8,24},{9,... | collective-permute-start | bytes 393224 | tf_op jit(solution)/shard_map/ppermute | solution.py:162
  185.8 3.1 %collective-permute-done.4 = bf16[2,1,128,256]{3,2,1,0:T(8,128)(2,1)S(1)} collective-permute-done((bf16[2,1,128,256]{3,2,1,0:T(8,128)(2,1)S(1)}, bf16[2,1,128,256]{3,2,1,0:T(8,128)(2,1)S(1)}, u32[]{:S(2)}, u32[]{:S(2)}) %collective-permute-start.4) | collective-permute-done | bytes 131104 | tf_op jit(solution)/shard_map/ppermute | solution.py:162
  189.2 0.7 fusion.224
  189.9 0.8 convolution_convert_fusion.2
  190.6 0.2 bitcast_dynamic-update-slice_fusion.9
  190.9 3.0 %collective-permute-start.5 = (bf16[128,256]{1,0:T(8,128)(2,1)S(1)}, bf16[128,256]{1,0:T(8,128)(2,1)S(1)}, u32[]{:S(2)}, u32[]{:S(2)}) collective-permute-start(bf16[128,256]{1,0:T(8,128)(2,1)S(1)} %get-tuple-element.6), channel_id=1, source_target_pairs={{0,2},{1,3},{2,0},{3,1},{4,6},{5,7},{6,4},{7,5},{8,10},{9,11},{10,... | collective-permute-start | bytes 196616 | tf_op jit(solution)/shard_map/ppermute | solution.py:162
  194.2 0.2 convolution_convert_fusion.7
  194.4 2.3 collective-permute-done.5
  196.7 3.1 %collective-permute-start.6 = (bf16[256,256]{1,0:T(8,128)(2,1)S(1)}, bf16[256,256]{1,0:T(8,128)(2,1)S(1)}, u32[]{:S(2)}, u32[]{:S(2)}) collective-permute-start(bf16[256,256]{1,0:T(8,128)(2,1)S(1)} %pad_maximum_fusion.7), channel_id=1, source_target_pairs={{0,16},{1,17},{2,18},{3,19},{4,20},{5,21},{6,22},{7,23},{8,24},{9,... | collective-permute-start | bytes 393224 | tf_op jit(solution)/shard_map/ppermute | solution.py:162
  199.8 0.6 bitcast_dynamic-update-slice_fusion.11
  200.6 2.7 collective-permute-done.6
  203.3 0.4 collective-permute-start.7
  203.7 0.6 bitcast_dynamic-update-slice_fusion.10
  204.4 5.4 %collective-permute-done.7 = bf16[512,256]{1,0:T(8,128)(2,1)S(1)} collective-permute-done((bf16[512,256]{1,0:T(8,128)(2,1)S(1)}, bf16[512,256]{1,0:T(8,128)(2,1)S(1)}, u32[]{:S(2)}, u32[]{:S(2)}) %collective-permute-start.7) | collective-permute-done | bytes 262176 | tf_op jit(solution)/shard_map/ppermute | solution.py:162
  209.8 2.0 collective-permute-start.8
  211.9 7.2 %collective-permute-done.8 = bf16[1024,256]{1,0:T(8,128)(2,1)S(1)} collective-permute-done((bf16[1024,256]{1,0:T(8,128)(2,1)S(1)}, bf16[1024,256]{1,0:T(8,128)(2,1)S(1)}, u32[]{:S(2)}, u32[]{:S(2)}) %collective-permute-start.8) | collective-permute-done | bytes 524320 | tf_op jit(solution)/shard_map/ppermute | solution.py:162
  219.1 1.6 collective-permute-start.9
  220.7 0.7 bitcast_dynamic-update-slice_fusion.7
  221.3 0.7 bitcast_dynamic-update-slice_fusion.5
  222.1 0.8 bitcast_dynamic-update-slice_fusion.3
  222.9 12.4 %collective-permute-done.9 = bf16[2048,256]{1,0:T(8,128)(2,1)S(1)} collective-permute-done((bf16[2048,256]{1,0:T(8,128)(2,1)S(1)}, bf16[2048,256]{1,0:T(8,128)(2,1)S(1)}, u32[]{:S(2)}, u32[]{:S(2)}) %collective-permute-start.9) | collective-permute-done | bytes 1048608 | tf_op jit(solution)/shard_map/ppermute | solution.py:162
  235.4 0.6 convert_reduce_fusion
  236.1 1.3 fusion.15
  237.5 3.9 %convolution_convert_fusion = bf16[4096,256]{0,1:T(8,128)(2,1)} fusion(bf16[3,256,256]{2,1,0:T(8,128)(2,1)S(1)} %copy-done.3, bf16[1,4096,1,1,1,1,256]{6,1,5,4,3,2,0:T(8,128)(2,1)S(1)} %bitcast_dynamic-update-slice_fusion.1, f32[4096]{0:T(1024)S(1)} %add_rsqrt_fusion, f32[4096]{0:T(1024)S(1)} %broadcast_multiply_fusion), kind=kOutput, calls=%fused_computation.18 | convolution fusion | flops 542113792 | bytes 4358144 | tf_op jit(solution)/shard_map/dot_general | solution.py:173
  241.4 1.9 convolution_convert_fusion.1
  243.3 9.6 %fusion.227 = (f32[8,128]{1,0:T(8,128)S(1)}, f32[8,128,4096]{2,1,0:T(8,128)}) fusion(bf16[128,8,32]{0,2,1:T(8,128)(2,1)S(1)} %bitcast.226, bf16[4096,8,32]{0,2,1:T(8,128)(2,1)} %bitcast.273), kind=kOutput, calls=%fused_computation.251 | convolution fusion | flops 281022464 | bytes 18944000 | tf_op jit(solution)/shard_map/sub | solution.py:189
  252.9 8.8 %fusion.37 = bf16[8,32,128]{2,1,0:T(8,128)(2,1)S(1)} fusion(bf16[4096,8,32]{0,2,1:T(8,128)(2,1)S(1)} %bitcast.272, f32[8,128,4096]{2,1,0:T(8,128)} %get-tuple-element.29, f32[8,128]{1,0:T(8,128)S(1)} %get-tuple-element.28), kind=kOutput, calls=%fused_computation.50 | convolution fusion | flops 276856832 | bytes 18944000 | tf_op jit(solution)/shard_map/bhqk,bkhd->bqhd/dot_general | solution.py:191
  261.6 8.1 %fusion.18.unpooled_hbm = f32[64,128,256]{2,1,0:T(8,128)} fusion(bf16[32,64,8,256]{3,2,1,0:T(8,128)(2,1)} %bitcast.213, f32[128,256]{1,0:T(8,128)S(1)} %get-tuple-element.27, bf16[128,256]{0,1:T(8,128)(2,1)S(1)} %bitcast.224, bf16[256,256]{1,0:T(8,128)(2,1)S(1)} %copy-done), kind=kOutput, calls=%fused_computation.25 | convolution fusion | flops 1090584576 | bytes 17104896 | tf_op jit(solution)/shard_map/rd,dje->jre/dot_general | solution.py:258
  269.7 15.7 %shard_map.136 = bf16[8192,256]{1,0:T(8,128)(2,1)} custom-call(s32[32]{0:T(128)} %counts_ref.3, f32[8192,256]{1,0:T(8,128)} %shard_map.135.refined_ref, f32[64,128,256]{2,1,0:T(8,128)} %fusion.18.unpooled_hbm), custom_call_target="tpu_custom_call" | custom-call | tf_op jit(solution)/shard_map/pallas_call | solution.py:139
  (98 shorter events, 6.9 us)
Async XLA Ops:
  0.0 261.6 %copy-start = (bf16[256,256]{1,0:T(8,128)(2,1)S(1)}, bf16[256,256]{1,0:T(8,128)(2,1)}, u32[]{:S(2)}) copy-start(bf16[256,256]{1,0:T(8,128)(2,1)} %param.22) | copy-start | bytes 393220
  98.0 10.0 %copy-start.1 = (bf16[3,256,256]{2,1,0:T(8,128)(2,1)S(1)}, bf16[3,256,256]{2,1,0:T(8,128)(2,1)}, u32[]{:S(2)}) copy-start(bf16[3,256,256]{2,1,0:T(8,128)(2,1)} %param.19) | copy-start | bytes 1179652
  108.4 45.5 %collective-permute-start = (bf16[2,1,128,256]{3,2,1,0:T(8,128)(2,1)S(1)}, bf16[2,1,128,256]{3,2,1,0:T(8,128)(2,1)S(1)}, u32[]{:S(2)}, u32[]{:S(2)}) collective-permute-start(bf16[2,1,128,256]{3,2,1,0:T(8,128)(2,1)S(1)} %pad_maximum_fusion.2), channel_id=1, source_target_pairs={{0,1},{1,0},{2,3},{3,2},{4,5},{5,4},{6,7},{7,6},{8,9},{9,8},{10,11... | collective-permute-start | bytes 393224 | tf_op jit(solution)/shard_map/ppermute | solution.py:162
  153.9 1.7 copy-start.2
  156.8 6.6 %collective-permute-start.1 = (bf16[2,1,128,256]{3,2,1,0:T(8,128)(2,1)S(1)}, bf16[2,1,128,256]{3,2,1,0:T(8,128)(2,1)S(1)}, u32[]{:S(2)}, u32[]{:S(2)}) collective-permute-start(bf16[2,1,128,256]{3,2,1,0:T(8,128)(2,1)S(1)} %pad_maximum_fusion.3), channel_id=1, source_target_pairs={{0,2},{1,3},{2,0},{3,1},{4,6},{5,7},{6,4},{7,5},{8,10},{9,11},{10,... | collective-permute-start | bytes 393224 | tf_op jit(solution)/shard_map/ppermute | solution.py:162
  166.3 5.0 %collective-permute-start.2 = (bf16[2,1,128,256]{3,2,1,0:T(8,128)(2,1)S(1)}, bf16[2,1,128,256]{3,2,1,0:T(8,128)(2,1)S(1)}, u32[]{:S(2)}, u32[]{:S(2)}) collective-permute-start(bf16[2,1,128,256]{3,2,1,0:T(8,128)(2,1)S(1)} %pad_maximum_fusion.4), channel_id=1, source_target_pairs={{0,4},{1,5},{2,6},{3,7},{4,0},{5,1},{6,2},{7,3},{8,12},{9,13},{10,... | collective-permute-start | bytes 393224 | tf_op jit(solution)/shard_map/ppermute | solution.py:162
  174.2 5.3 %collective-permute-start.3 = (bf16[2,1,128,256]{3,2,1,0:T(8,128)(2,1)S(1)}, bf16[2,1,128,256]{3,2,1,0:T(8,128)(2,1)S(1)}, u32[]{:S(2)}, u32[]{:S(2)}) collective-permute-start(bf16[2,1,128,256]{3,2,1,0:T(8,128)(2,1)S(1)} %pad_maximum_fusion.5), channel_id=1, source_target_pairs={{0,8},{1,9},{2,10},{3,11},{4,12},{5,13},{6,14},{7,15},{8,0},{9,1},... | collective-permute-start | bytes 393224 | tf_op jit(solution)/shard_map/ppermute | solution.py:162
  182.1 12.0 %copy-start.3 = (bf16[3,256,256]{2,1,0:T(8,128)(2,1)S(1)}, bf16[3,256,256]{2,1,0:T(8,128)(2,1)}, u32[]{:S(2)}) copy-start(bf16[3,256,256]{2,1,0:T(8,128)(2,1)} %param.21) | copy-start | bytes 1179652
  182.4 6.6 %collective-permute-start.4 = (bf16[2,1,128,256]{3,2,1,0:T(8,128)(2,1)S(1)}, bf16[2,1,128,256]{3,2,1,0:T(8,128)(2,1)S(1)}, u32[]{:S(2)}, u32[]{:S(2)}) collective-permute-start(bf16[2,1,128,256]{3,2,1,0:T(8,128)(2,1)S(1)} %pad_maximum_fusion.6), channel_id=1, source_target_pairs={{0,16},{1,17},{2,18},{3,19},{4,20},{5,21},{6,22},{7,23},{8,24},{9,... | collective-permute-start | bytes 393224 | tf_op jit(solution)/shard_map/ppermute | solution.py:162
  190.9 5.8 %collective-permute-start.5 = (bf16[128,256]{1,0:T(8,128)(2,1)S(1)}, bf16[128,256]{1,0:T(8,128)(2,1)S(1)}, u32[]{:S(2)}, u32[]{:S(2)}) collective-permute-start(bf16[128,256]{1,0:T(8,128)(2,1)S(1)} %get-tuple-element.6), channel_id=1, source_target_pairs={{0,2},{1,3},{2,0},{3,1},{4,6},{5,7},{6,4},{7,5},{8,10},{9,11},{10,... | collective-permute-start | bytes 196616 | tf_op jit(solution)/shard_map/ppermute | solution.py:162
  196.7 6.6 %collective-permute-start.6 = (bf16[256,256]{1,0:T(8,128)(2,1)S(1)}, bf16[256,256]{1,0:T(8,128)(2,1)S(1)}, u32[]{:S(2)}, u32[]{:S(2)}) collective-permute-start(bf16[256,256]{1,0:T(8,128)(2,1)S(1)} %pad_maximum_fusion.7), channel_id=1, source_target_pairs={{0,16},{1,17},{2,18},{3,19},{4,20},{5,21},{6,22},{7,23},{8,24},{9,... | collective-permute-start | bytes 393224 | tf_op jit(solution)/shard_map/ppermute | solution.py:162
  203.3 6.5 %collective-permute-start.7 = (bf16[512,256]{1,0:T(8,128)(2,1)S(1)}, bf16[512,256]{1,0:T(8,128)(2,1)S(1)}, u32[]{:S(2)}, u32[]{:S(2)}) collective-permute-start(bf16[512,256]{1,0:T(8,128)(2,1)S(1)} %pad_maximum_fusion.1), channel_id=1, source_target_pairs={{0,1},{1,0},{2,3},{3,2},{4,5},{5,4},{6,7},{7,6},{8,9},{9,8},{10,11... | collective-permute-start | bytes 786440 | tf_op jit(solution)/shard_map/ppermute | solution.py:162
  209.8 9.3 %collective-permute-start.8 = (bf16[1024,256]{1,0:T(8,128)(2,1)S(1)}, bf16[1024,256]{1,0:T(8,128)(2,1)S(1)}, u32[]{:S(2)}, u32[]{:S(2)}) collective-permute-start(bf16[1024,256]{1,0:T(8,128)(2,1)S(1)} %pad_maximum_fusion), channel_id=1, source_target_pairs={{0,4},{1,5},{2,6},{3,7},{4,0},{5,1},{6,2},{7,3},{8,12},{9,13},{10,... | collective-permute-start | bytes 1572872 | tf_op jit(solution)/shard_map/ppermute | solution.py:162
  219.1 16.3 %collective-permute-start.9 = (bf16[2048,256]{1,0:T(8,128)(2,1)S(1)}, bf16[2048,256]{1,0:T(8,128)(2,1)S(1)}, u32[]{:S(2)}, u32[]{:S(2)}) collective-permute-start(bf16[2048,256]{1,0:T(8,128)(2,1)S(1)} %constant_dynamic-update-slice_fusion), channel_id=1, source_target_pairs={{0,8},{1,9},{2,10},{3,11},{4,12},{5,13},{6,14},{7,15},{8,0},{9,1},... | collective-permute-start | bytes 3145736 | tf_op jit(solution)/shard_map/ppermute | solution.py:162
  222.9 14.4 %copy-start.4 = (bf16[1,4096,1,1,1,1,256]{6,1,5,4,3,2,0:T(8,128)(2,1)S(1)}, bf16[1,4096,1,1,1,1,256]{6,1,5,4,3,2,0:T(8,128)(2,1)}, u32[]{:S(2)}) copy-start(bf16[1,4096,1,1,1,1,256]{6,1,5,4,3,2,0:T(8,128)(2,1)} %bitcast_dynamic-update-slice_fusion.3) | copy-start | bytes 6291460

commit v5 on v4

--- a/solution.py
+++ b/solution.py
@@ -16,6 +16,10 @@
 EPSILON = 1e-05
 GATHER_ORDER = (1, 4, 0, 2, 3)
 MLP_CHUNK_ROWS = 1024
+MLP_BLOCK_ROWS = 256
+BALLS_PER_STEP = 2
+FINAL_TOKENS_PER_STEP = 16
+GLOBAL_UNROLL = 2
 
 
 def _norm(x):
@@ -25,47 +29,59 @@
 
 
 def _ball_kernel(counts_ref, x_ref, proj_ref, wo_ref, masked_ref):
-    count = counts_ref[pl.program_id(0)]
+    rows, feature = x_ref.shape
+    balls = rows // BALL
+    first_ball = pl.program_id(0) * balls
     x = x_ref[...].astype(jnp.float32)
-    feature = x.shape[-1]
     head_size = feature // HEADS
     normed = _norm(x)
     q = jnp.dot(normed, proj_ref[0], preferred_element_type=jnp.float32).astype(jnp.bfloat16)
     k = jnp.dot(normed, proj_ref[1], preferred_element_type=jnp.float32).astype(jnp.bfloat16)
     v = jnp.dot(normed, proj_ref[2], preferred_element_type=jnp.float32).astype(jnp.bfloat16)
-    k_t = k.T
-    key_live = lax.broadcasted_iota(jnp.int32, (1, BALL), 1) < count
     lane = lax.broadcasted_iota(jnp.int32, (1, feature), 1)
     scale = 1.0 / math.sqrt(head_size)
-    mixed = jnp.zeros((BALL, feature), jnp.float32)
-    for h in range(HEADS):
-        in_head = (lane >= h * head_size) & (lane < (h + 1) * head_size)
-        qh = jnp.where(in_head, q, jnp.zeros((), jnp.bfloat16))
-        vh = jnp.where(in_head, v, jnp.zeros((), jnp.bfloat16))
-        scores = jnp.dot(qh, k_t, preferred_element_type=jnp.float32) * scale
-        scores = jnp.where(key_live, scores, -1e30)
-        row_max = jnp.max(scores, axis=-1, keepdims=True)
-        expo = jnp.exp(scores - row_max)
-        probs = (expo * (1.0 / jnp.sum(expo, axis=-1, keepdims=True))).astype(jnp.bfloat16)
-        mixed = mixed + jnp.dot(probs, vh, preferred_element_type=jnp.float32)
-    mixed = mixed.astype(jnp.bfloat16)
+    mixed_balls = []
+    for ball in range(balls):
+        count = counts_ref[first_ball + ball]
+        own = slice(ball * BALL, (ball + 1) * BALL)
+        q_ball, v_ball = q[own], v[own]
+        k_t = k[own].T
+        key_live = lax.broadcasted_iota(jnp.int32, (1, BALL), 1) < count
+
+        def head(h, mixed):
+            in_head = (lane >= h * head_size) & (lane < (h + 1) * head_size)
+            qh = jnp.where(in_head, q_ball, jnp.zeros((), jnp.bfloat16))
+            vh = jnp.where(in_head, v_ball, jnp.zeros((), jnp.bfloat16))
+            scores = jnp.dot(qh, k_t, preferred_element_type=jnp.float32) * scale
+            scores = jnp.where(key_live, scores, -1e30)
+            row_max = jnp.max(scores, axis=-1, keepdims=True)
+            expo = jnp.exp(scores - row_max)
+            probs = (expo * (1.0 / jnp.sum(expo, axis=-1, keepdims=True))).astype(jnp.bfloat16)
+            return mixed + jnp.dot(probs, vh, preferred_element_type=jnp.float32)
+
+        mixed = lax.fori_loop(0, HEADS, head, jnp.zeros((BALL, feature), jnp.float32), unroll=True)
+        mixed_balls.append(mixed.astype(jnp.bfloat16))
+    mixed = jnp.concatenate(mixed_balls, axis=0) if balls > 1 else mixed_balls[0]
     fine = (x + jnp.dot(mixed, wo_ref[...], preferred_element_type=jnp.float32)).astype(jnp.bfloat16)
-    row_live = lax.broadcasted_iota(jnp.int32, (BALL, 1), 0) < count
-    masked_ref[...] = jnp.where(row_live, fine, jnp.zeros((), jnp.bfloat16))
+    row = lax.broadcasted_iota(jnp.int32, (rows, 1), 0)
+    count_of_row = jnp.zeros((rows, 1), jnp.int32)
+    for ball in range(balls):
+        count_of_row = jnp.where(row // BALL == ball, counts_ref[first_ball + ball], count_of_row)
+    masked_ref[...] = jnp.where(row % BALL < count_of_row, fine, jnp.zeros((), jnp.bfloat16))
 
 
 def ball_block(tree_rows, ball_counts, ball_proj, ball_out):
     rows, feature = tree_rows.shape
-    balls = rows // BALL
+    block = BALLS_PER_STEP * BALL
     return pl.pallas_call(
         _ball_kernel,
         out_shape=jax.ShapeDtypeStruct((rows, feature), jnp.bfloat16),
         grid_spec=pltpu.PrefetchScalarGridSpec(
-            num_scalar_prefetch=1, grid=(balls,),
-            in_specs=[pl.BlockSpec((BALL, feature), lambda i, c: (i, 0)),
+            num_scalar_prefetch=1, grid=(rows // block,),
+            in_specs=[pl.BlockSpec((block, feature), lambda i, c: (i, 0)),
                       pl.BlockSpec((3, feature, feature), lambda i, c: (0, 0, 0)),
                       pl.BlockSpec((feature, feature), lambda i, c: (0, 0))],
-            out_specs=pl.BlockSpec((BALL, feature), lambda i, c: (i, 0))),
+            out_specs=pl.BlockSpec((block, feature), lambda i, c: (i, 0))),
         compiler_params=pltpu.CompilerParams(dimension_semantics=("arbitrary",)),
     )(ball_counts, tree_rows, ball_proj, ball_out)
 
@@ -80,7 +96,7 @@
 def mlp_block(fine, refined, first_block, block_count, mlp_in, mlp_out):
     rows, feature = fine.shape
     ff = mlp_in.shape[1]
-    in_specs = [pl.BlockSpec((BALL, feature), lambda i: (first_block + i, 0)),
+    in_specs = [pl.BlockSpec((MLP_BLOCK_ROWS, feature), lambda i: (first_block + i, 0)),
                 pl.BlockSpec((feature, ff), lambda i: (0, 0)),
                 pl.BlockSpec((ff, feature), lambda i: (0, 0))]
     operands = [fine, mlp_in, mlp_out]
@@ -95,7 +111,7 @@
         out_shape=jax.ShapeDtypeStruct((rows, feature), jnp.float32),
         grid=(block_count,),
         in_specs=in_specs,
-        out_specs=pl.BlockSpec((BALL, feature), lambda i: (first_block + i, 0)),
+        out_specs=pl.BlockSpec((MLP_BLOCK_ROWS, feature), lambda i: (first_block + i, 0)),
         input_output_aliases=aliases,
         compiler_params=pltpu.CompilerParams(dimension_semantics=("arbitrary",)),
     )(*operands)
@@ -135,7 +151,7 @@
 def final_block(ball_counts, refined, unpooled):
     rows, feature = refined.shape
     slots, tokens, _ = unpooled.shape
-    per_step = 8
+    per_step = FINAL_TOKENS_PER_STEP
     return pl.pallas_call(
         _final_kernel,
         out_shape=jax.ShapeDtypeStruct((rows, feature), jnp.bfloat16),
@@ -148,6 +164,39 @@
                             pltpu.SemaphoreType.DMA((2,))]),
         compiler_params=pltpu.CompilerParams(dimension_semantics=("arbitrary",)),
     )(ball_counts, refined, unpooled)
+
+
+def _global_kernel(state_ref, everyone_ref, proj_ref, wo_ref, summary_ref):
+    state = state_ref[...]
+    feature = state.shape[-1]
+    head_size = feature // HEADS
+    q = jnp.dot(_norm(state), proj_ref[0], preferred_element_type=jnp.float32).astype(jnp.bfloat16)
+    normed_all = _norm(everyone_ref[...].astype(jnp.float32))
+    k_t = jnp.dot(normed_all, proj_ref[1], preferred_element_type=jnp.float32).astype(jnp.bfloat16).T
+    v = jnp.dot(normed_all, proj_ref[2], preferred_element_type=jnp.float32).astype(jnp.bfloat16)
+    lane = lax.broadcasted_iota(jnp.int32, (1, feature), 1)
+    scale = 1.0 / math.sqrt(head_size)
+
+    def head(h, mixed):
+        in_head = (lane >= h * head_size) & (lane < (h + 1) * head_size)
+        qh = jnp.where(in_head, q, jnp.zeros((), jnp.bfloat16))
+        vh = jnp.where(in_head, v, jnp.zeros((), jnp.bfloat16))
+        scores = jnp.dot(qh, k_t, preferred_element_type=jnp.float32) * scale
+        row_max = jnp.max(scores, axis=-1, keepdims=True)
+        expo = jnp.exp(scores - row_max)
+        probs = (expo * (1.0 / jnp.sum(expo, axis=-1, keepdims=True))).astype(jnp.bfloat16)
+        return mixed + jnp.dot(probs, vh, preferred_element_type=jnp.float32)
+
+    mixed = lax.fori_loop(0, HEADS, head, jnp.zeros(state.shape, jnp.float32), unroll=GLOBAL_UNROLL).astype(jnp.bfloat16)
+    summary_ref[...] = (state + jnp.dot(mixed, wo_ref[...], preferred_element_type=jnp.float32)).astype(
+        summary_ref.dtype)
+
+
+def global_block(state, everyone, global_proj, global_out):
+    return pl.pallas_call(
+        _global_kernel,
+        out_shape=jax.ShapeDtypeStruct(state.shape, jnp.bfloat16),
+    )(state, everyone, global_proj, global_out)
 
 
 def gather_all(shard, axis, order):
@@ -225,7 +274,7 @@
     chunk = MLP_CHUNK_ROWS
     refined = None
     for start in range(0, row_count, chunk):
-        refined = mlp_block(masked, refined, start // BALL, chunk // BALL, mlp_in, mlp_out)
+        refined = mlp_block(masked, refined, start // MLP_BLOCK_ROWS, chunk // MLP_BLOCK_ROWS, mlp_in, mlp_out)
     pooled = jnp.einsum(
         "rjd,jde->re",
         masked.reshape(row_count // POOL, POOL, feature),
@@ -245,16 +294,8 @@
             jnp.concatenate([value_rows, received[1]], axis=1),
             coarse_out,
         )
-    normed = normalize(coarse_state)
-    queries = project(normed, global_proj[0])
-    everyone = gather_all(coarse_state[0].astype(jnp.bfloat16), "point", GATHER_ORDER)[None]
-    normed_all = normalize(everyone)
-    all_keys = project(normed_all, global_proj[1])
-    all_values = project(normed_all, global_proj[2])
-    mixed = attend(queries, all_keys, all_values, None, HEADS)
-    summary = (
-        coarse_state + jnp.dot(mixed, global_out, preferred_element_type=jnp.float32)
-    ).astype(jnp.bfloat16)
+    everyone = gather_all(coarse_state[0].astype(jnp.bfloat16), "point", GATHER_ORDER)
+    summary = global_block(coarse_state[0], everyone, global_proj, global_out)
     unpooled = jnp.einsum(
         "rd,dje->jre",
         summary.reshape(-1, feature),

time: 287 us -> 254 us (0.89)
  matrix products: 53 us -> 29.1 us
  waiting for transfers between devices: 42.3 us -> 30.2 us
  Pallas kernels: 122 us -> 125 us
    pallas_call x0 -> x1, Pallas kernels: none -> 19.5 us  [global_block(): pl.pallas_call(_global_kernel, out_shape=jax.ShapeDtypeStruct(state.shape...]
    ppermute x10, waiting for transfers between devices: 42.3 us -> 30.2 us  [partner(): lax.ppermute(shard, axis, [(i, i ^ 1 << apart) for i in range(lax.axis_si...]
    pallas_call x1, Pallas kernels: 63.3 us -> 51.3 us  [ball_block(): pl.pallas_call(_ball_kernel, out_shape=jax.ShapeDtypeStruct((rows, featur...]
    sub x6 -> x5, matrix products: 12.8 us -> 3.25 us  [attend(): expo = jnp.exp(scores - row_max)]
    dot_general x6 -> x5, matrix products: 12.6 us -> 3.83 us  [attend(): jnp.einsum('bhqk,bkhd->bqhd', attn_probs, v_heads, preferred_element_type...]
    dot_general x18 -> x15, matrix products: 8.4 us -> 2.38 us  [project(): jnp.dot(inputs, weight, preferred_element_type=jnp.float32)]
    pallas_call x1, Pallas kernels: 15.7 us -> 11.5 us  [final_block(): pl.pallas_call(_final_kernel, out_shape=jax.ShapeDtypeStruct((rows, featu...]
  transfers between devices with their start and end apart: 10 -> 10, of which waited for: 9 -> 9; matrix products, arithmetic and copies ran while one was open for 2% -> 1% of each run, Pallas kernels for 15% -> 17%
where the time goes in v5:
time: 254 us; the launch traced here: 253 us
  Pallas kernels  125 us (49%)
  local copies, waits for them, and re-layouts  41.1 us (16%)
  waiting for transfers between devices  30.2 us (12%)
  matrix products  29.1 us (11%)
  starting transfers between devices  24.4 us (10%)
    pallas_call x1, Pallas kernels, ball_block(): pl.pallas_call(_ball_kernel, out_shape=jax.ShapeDtypeStruct((rows, featur...  51.3 us
    pallas_call x8, Pallas kernels, mlp_block(): pl.pallas_call(kernel, out_shape=jax.ShapeDtypeStruct((rows, feature), jn...  42.9 us
    gather x1, local copies, waits for them, and re-layouts, local_body(): points.at[tree_order - offset]  33.9 us
    ppermute x10, waiting for transfers between devices, partner(): lax.ppermute(shard, axis, [(i, i ^ 1 << apart) for i in range(lax.axis_si...  30.2 us
    ppermute x10, starting transfers between devices, partner(): lax.ppermute(shard, axis, [(i, i ^ 1 << apart) for i in range(lax.axis_si...  24.4 us
    pallas_call x1, Pallas kernels, global_block(): pl.pallas_call(_global_kernel, out_shape=jax.ShapeDtypeStruct(state.shape...  19.5 us
    pallas_call x1, Pallas kernels, final_block(): pl.pallas_call(_final_kernel, out_shape=jax.ShapeDtypeStruct((rows, featu...  11.5 us
    dot_general x1, matrix products, local_body(): jnp.einsum('rjd,jde->re', masked.reshape(row_count // POOL, POOL, feature...  9.66 us
  transfers between devices with their start and end apart: 10, of which 9 were waited for; matrix products, arithmetic and copies ran while one was open for 1% of the time, Pallas kernels for 17%

profile of v5, /device:TPU:0, one launch (start us, length us, event | category | flops | bytes accessed | tf_op | source)
XLA Modules:
  0.0 253.3 jit_solution(11279209271209006073)
XLA Ops:
  0.0 0.8 fusion.112
  0.8 33.9 %gather_fusion = bf16[8192,256]{1,0:T(8,128)(2,1)} fusion(bf16[8192,256]{1,0:T(8,128)(2,1)} %param.13, s32[8192]{0:T(1024)S(1)} %fusion.112), kind=kCustom, calls=%fused_computation | custom fusion | bytes 8421376 | tf_op jit(solution)/shard_map/gather | solution.py:271
  34.7 51.3 %shard_map.127.fine_ref.f = bf16[8192,256]{1,0:T(8,128)(2,1)} custom-call(s32[32]{0:T(128)} %counts_ref.3, bf16[8192,256]{1,0:T(8,128)(2,1)} %gather_fusion, bf16[3,256,256]{2,1,0:T(8,128)(2,1)} %proj_ref.2, bf16[256,256]{1,0:T(8,128)(2,1)} %wo_ref.2), custom_call_target="tpu_custom_call" | custom-call | tf_op jit(solution)/shard_map/pallas_call | solution.py:76
  86.0 9.7 %fusion.183 = (f32[128]{0:T(128)S(1)}, f32[128,256]{1,0:T(8,128)S(1)}) fusion(bf16[64,256,256]{2,1,0:T(8,128)(2,1)} %bitcast.216, bf16[128,64,256]{2,1,0:T(8,128)(2,1)} %bitcast.159), kind=kOutput, calls=%fused_computation.200 | convolution fusion | flops 1073774464 | bytes 12714496 | tf_op jit(solution)/shard_map/rjd,jde->re/dot_general | solution.py:278
  95.6 0.2 multiply_reduce_fusion.4
  96.1 0.2 convolution_convert_fusion.18
  96.3 1.8 collective-permute-start
  98.3 0.2 convolution_convert_fusion.17
  98.6 3.0 %collective-permute-done = bf16[2,1,128,256]{3,2,1,0:T(8,128)(2,1)S(1)} collective-permute-done((bf16[2,1,128,256]{3,2,1,0:T(8,128)(2,1)S(1)}, bf16[2,1,128,256]{3,2,1,0:T(8,128)(2,1)S(1)}, u32[]{:S(2)}, u32[]{:S(2)}) %collective-permute-start) | collective-permute-done | bytes 131104 | tf_op jit(solution)/shard_map/ppermute | solution.py:211
  101.8 0.7 fusion.184
  102.5 0.8 convolution_convert_fusion.4
  103.3 0.3 fusion.187
  103.6 0.2 multiply_reduce_fusion.3
  104.1 0.2 convolution_convert_fusion.15
  104.5 3.6 %collective-permute-start.1 = (bf16[2,1,128,256]{3,2,1,0:T(8,128)(2,1)S(1)}, bf16[2,1,128,256]{3,2,1,0:T(8,128)(2,1)S(1)}, u32[]{:S(2)}, u32[]{:S(2)}) collective-permute-start(bf16[2,1,128,256]{3,2,1,0:T(8,128)(2,1)S(1)} %pad_maximum_fusion.3), channel_id=1, source_target_pairs={{0,2},{1,3},{2,0},{3,1},{4,6},{5,7},{6,4},{7,5},{8,10},{9,11},{10,... | collective-permute-start | bytes 393224 | tf_op jit(solution)/shard_map/ppermute | solution.py:211
  108.4 2.8 %collective-permute-done.1 = bf16[2,1,128,256]{3,2,1,0:T(8,128)(2,1)S(1)} collective-permute-done((bf16[2,1,128,256]{3,2,1,0:T(8,128)(2,1)S(1)}, bf16[2,1,128,256]{3,2,1,0:T(8,128)(2,1)S(1)}, u32[]{:S(2)}, u32[]{:S(2)}) %collective-permute-start.1) | collective-permute-done | bytes 131104 | tf_op jit(solution)/shard_map/ppermute | solution.py:211
  111.5 0.6 fusion.188
  112.1 0.8 convolution_convert_fusion.3
  112.9 0.3 fusion.191
  113.2 0.2 multiply_reduce_fusion.2
  113.7 0.2 convolution_convert_fusion.12
  114.1 2.2 collective-permute-start.2
  116.6 2.7 %collective-permute-done.2 = bf16[2,1,128,256]{3,2,1,0:T(8,128)(2,1)S(1)} collective-permute-done((bf16[2,1,128,256]{3,2,1,0:T(8,128)(2,1)S(1)}, bf16[2,1,128,256]{3,2,1,0:T(8,128)(2,1)S(1)}, u32[]{:S(2)}, u32[]{:S(2)}) %collective-permute-start.2) | collective-permute-done | bytes 131104 | tf_op jit(solution)/shard_map/ppermute | solution.py:211
  119.5 0.7 fusion.192
  120.2 0.8 convolution_convert_fusion.2
  120.9 0.3 fusion.195
  121.2 0.2 multiply_reduce_fusion.1
  121.7 0.2 convolution_convert_fusion.9
  122.2 1.7 collective-permute-start.3
  124.1 3.1 %collective-permute-done.3 = bf16[2,1,128,256]{3,2,1,0:T(8,128)(2,1)S(1)} collective-permute-done((bf16[2,1,128,256]{3,2,1,0:T(8,128)(2,1)S(1)}, bf16[2,1,128,256]{3,2,1,0:T(8,128)(2,1)S(1)}, u32[]{:S(2)}, u32[]{:S(2)}) %collective-permute-start.3) | collective-permute-done | bytes 131104 | tf_op jit(solution)/shard_map/ppermute | solution.py:211
  127.5 0.6 fusion.196
  128.1 0.8 convolution_convert_fusion.1
  128.9 0.3 fusion.199
  129.2 0.2 multiply_reduce_fusion
  130.1 3.2 %collective-permute-start.4 = (bf16[2,1,128,256]{3,2,1,0:T(8,128)(2,1)S(1)}, bf16[2,1,128,256]{3,2,1,0:T(8,128)(2,1)S(1)}, u32[]{:S(2)}, u32[]{:S(2)}) collective-permute-start(bf16[2,1,128,256]{3,2,1,0:T(8,128)(2,1)S(1)} %pad_maximum_fusion.6), channel_id=1, source_target_pairs={{0,16},{1,17},{2,18},{3,19},{4,20},{5,21},{6,22},{7,23},{8,24},{9,... | collective-permute-start | bytes 393224 | tf_op jit(solution)/shard_map/ppermute | solution.py:211
  133.6 3.1 %collective-permute-done.4 = bf16[2,1,128,256]{3,2,1,0:T(8,128)(2,1)S(1)} collective-permute-done((bf16[2,1,128,256]{3,2,1,0:T(8,128)(2,1)S(1)}, bf16[2,1,128,256]{3,2,1,0:T(8,128)(2,1)S(1)}, u32[]{:S(2)}, u32[]{:S(2)}) %collective-permute-start.4) | collective-permute-done | bytes 131104 | tf_op jit(solution)/shard_map/ppermute | solution.py:211
  136.9 0.7 fusion.200
  137.6 0.8 convolution_convert_fusion
  138.3 0.9 constant_dynamic-update-slice_fusion.4
  139.2 3.3 %collective-permute-start.5 = (bf16[128,256]{1,0:T(8,128)(2,1)S(1)}, bf16[128,256]{1,0:T(8,128)(2,1)S(1)}, u32[]{:S(2)}, u32[]{:S(2)}) collective-permute-start(bf16[128,256]{1,0:T(8,128)(2,1)S(1)} %get-tuple-element.6), channel_id=1, source_target_pairs={{0,2},{1,3},{2,0},{3,1},{4,6},{5,7},{6,4},{7,5},{8,10},{9,11},{10,... | collective-permute-start | bytes 196616 | tf_op jit(solution)/shard_map/ppermute | solution.py:211
  142.5 2.5 collective-permute-done.5
  145.0 3.2 %collective-permute-start.6 = (bf16[256,256]{1,0:T(8,128)(2,1)S(1)}, bf16[256,256]{1,0:T(8,128)(2,1)S(1)}, u32[]{:S(2)}, u32[]{:S(2)}) collective-permute-start(bf16[256,256]{1,0:T(8,128)(2,1)S(1)} %pad_maximum_fusion.7), channel_id=1, source_target_pairs={{0,16},{1,17},{2,18},{3,19},{4,20},{5,21},{6,22},{7,23},{8,24},{9,... | collective-permute-start | bytes 393224 | tf_op jit(solution)/shard_map/ppermute | solution.py:211
  148.2 3.3 %collective-permute-done.6 = bf16[256,256]{1,0:T(8,128)(2,1)S(1)} collective-permute-done((bf16[256,256]{1,0:T(8,128)(2,1)S(1)}, bf16[256,256]{1,0:T(8,128)(2,1)S(1)}, u32[]{:S(2)}, u32[]{:S(2)}) %collective-permute-start.6) | collective-permute-done | bytes 131104 | tf_op jit(solution)/shard_map/ppermute | solution.py:211
  151.6 1.7 collective-permute-start.7
  153.3 4.7 %collective-permute-done.7 = bf16[512,256]{1,0:T(8,128)(2,1)S(1)} collective-permute-done((bf16[512,256]{1,0:T(8,128)(2,1)S(1)}, bf16[512,256]{1,0:T(8,128)(2,1)S(1)}, u32[]{:S(2)}, u32[]{:S(2)}) %collective-permute-start.7) | collective-permute-done | bytes 262176 | tf_op jit(solution)/shard_map/ppermute | solution.py:211
  158.1 2.1 collective-permute-start.8
  160.2 0.6 constant_dynamic-update-slice_fusion.3
  160.8 0.7 constant_dynamic-update-slice_fusion.2
  161.5 0.7 constant_dynamic-update-slice_fusion.1
  162.2 5.1 %collective-permute-done.8 = bf16[1024,256]{1,0:T(8,128)(2,1)S(1)} collective-permute-done((bf16[1024,256]{1,0:T(8,128)(2,1)S(1)}, bf16[1024,256]{1,0:T(8,128)(2,1)S(1)}, u32[]{:S(2)}, u32[]{:S(2)}) %collective-permute-start.8) | collective-permute-done | bytes 524320 | tf_op jit(solution)/shard_map/ppermute | solution.py:211
  167.3 0.9 constant_dynamic-update-slice_fusion
  168.2 1.6 collective-permute-start.9
  169.8 5.4 %shard_map.128._ = f32[8192,256]{1,0:T(8,128)} custom-call(bf16[8192,256]{1,0:T(8,128)(2,1)} %shard_map.127.fine_ref.f, bf16[256,1024]{1,0:T(8,128)(2,1)} %w1.13, bf16[1024,256]{1,0:T(8,128)(2,1)} %w2.13), custom_call_target="tpu_custom_call" | custom-call | tf_op jit(solution)/shard_map/pallas_call | solution.py:109
  175.2 5.4 %shard_map.129._ = f32[8192,256]{1,0:T(8,128)} custom-call(bf16[8192,256]{1,0:T(8,128)(2,1)} %shard_map.127.fine_ref.f, bf16[256,1024]{1,0:T(8,128)(2,1)} %w1.13, bf16[1024,256]{1,0:T(8,128)(2,1)} %w2.13, f32[8192,256]{1,0:T(8,128)} %shard_map.128._), custom_call_target="tpu_custom_call", output_to_operand_aliasing={{}: (3, {})} | custom-call | tf_op jit(solution)/shard_map/pallas_call | solution.py:109
  180.6 5.4 %shard_map.130._ = f32[8192,256]{1,0:T(8,128)} custom-call(bf16[8192,256]{1,0:T(8,128)(2,1)} %shard_map.127.fine_ref.f, bf16[256,1024]{1,0:T(8,128)(2,1)} %w1.13, bf16[1024,256]{1,0:T(8,128)(2,1)} %w2.13, f32[8192,256]{1,0:T(8,128)} %shard_map.129._), custom_call_target="tpu_custom_call", output_to_operand_aliasing={{}: (3, {})} | custom-call | tf_op jit(solution)/shard_map/pallas_call | solution.py:109
  185.9 5.4 %shard_map.131._ = f32[8192,256]{1,0:T(8,128)} custom-call(bf16[8192,256]{1,0:T(8,128)(2,1)} %shard_map.127.fine_ref.f, bf16[256,1024]{1,0:T(8,128)(2,1)} %w1.13, bf16[1024,256]{1,0:T(8,128)(2,1)} %w2.13, f32[8192,256]{1,0:T(8,128)} %shard_map.130._), custom_call_target="tpu_custom_call", output_to_operand_aliasing={{}: (3, {})} | custom-call | tf_op jit(solution)/shard_map/pallas_call | solution.py:109
  191.3 5.4 %shard_map.132._ = f32[8192,256]{1,0:T(8,128)} custom-call(bf16[8192,256]{1,0:T(8,128)(2,1)} %shard_map.127.fine_ref.f, bf16[256,1024]{1,0:T(8,128)(2,1)} %w1.13, bf16[1024,256]{1,0:T(8,128)(2,1)} %w2.13, f32[8192,256]{1,0:T(8,128)} %shard_map.131._), custom_call_target="tpu_custom_call", output_to_operand_aliasing={{}: (3, {})} | custom-call | tf_op jit(solution)/shard_map/pallas_call | solution.py:109
  196.6 5.4 %shard_map.133._ = f32[8192,256]{1,0:T(8,128)} custom-call(bf16[8192,256]{1,0:T(8,128)(2,1)} %shard_map.127.fine_ref.f, bf16[256,1024]{1,0:T(8,128)(2,1)} %w1.13, bf16[1024,256]{1,0:T(8,128)(2,1)} %w2.13, f32[8192,256]{1,0:T(8,128)} %shard_map.132._), custom_call_target="tpu_custom_call", output_to_operand_aliasing={{}: (3, {})} | custom-call | tf_op jit(solution)/shard_map/pallas_call | solution.py:109
  202.0 5.4 %shard_map.134._ = f32[8192,256]{1,0:T(8,128)} custom-call(bf16[8192,256]{1,0:T(8,128)(2,1)} %shard_map.127.fine_ref.f, bf16[256,1024]{1,0:T(8,128)(2,1)} %w1.13, bf16[1024,256]{1,0:T(8,128)(2,1)} %w2.13, f32[8192,256]{1,0:T(8,128)} %shard_map.133._), custom_call_target="tpu_custom_call", output_to_operand_aliasing={{}: (3, {})} | custom-call | tf_op jit(solution)/shard_map/pallas_call | solution.py:109
  207.4 5.4 %shard_map.135.refined_ref = f32[8192,256]{1,0:T(8,128)} custom-call(bf16[8192,256]{1,0:T(8,128)(2,1)} %shard_map.127.fine_ref.f, bf16[256,1024]{1,0:T(8,128)(2,1)} %w1.13, bf16[1024,256]{1,0:T(8,128)(2,1)} %w2.13, f32[8192,256]{1,0:T(8,128)} %shard_map.134._), custom_call_target="tpu_custom_call", output_to_operand_aliasing={{}: (3, {})} | custom-call | tf_op jit(solution)/shard_map/pallas_call | solution.py:109
  212.8 1.3 copy-done.2
  214.1 19.5 %shard_map.136 = bf16[128,256]{1,0:T(8,128)(2,1)} custom-call(f32[128,256]{1,0:T(8,128)} %get-tuple-element.35.state_ref, bf16[4096,256]{1,0:T(8,128)(2,1)} %copy-done.2, bf16[3,256,256]{2,1,0:T(8,128)(2,1)} %proj_ref.3, bf16[256,256]{1,0:T(8,128)(2,1)} %wo_ref.3), custom_call_target="tpu_custom_call" | custom-call | tf_op jit(solution)/shard_map/pallas_call | solution.py:196
  233.7 7.9 %fusion.10.unpooled_hbm = f32[64,128,256]{2,1,0:T(8,128)} fusion(bf16[32,64,8,256]{3,2,1,0:T(8,128)(2,1)} %bitcast.160, bf16[128,256]{1,0:T(8,128)(2,1)} %shard_map.136), kind=kOutput, calls=%fused_computation.11 | convolution fusion | flops 1073741824 | bytes 16842752 | tf_op jit(solution)/shard_map/rd,dje->jre/dot_general | solution.py:299
  241.6 11.5 %shard_map.137 = bf16[8192,256]{1,0:T(8,128)(2,1)} custom-call(s32[32]{0:T(128)} %counts_ref.3, f32[8192,256]{1,0:T(8,128)} %shard_map.135.refined_ref, f32[64,128,256]{2,1,0:T(8,128)} %fusion.10.unpooled_hbm), custom_call_target="tpu_custom_call" | custom-call | tf_op jit(solution)/shard_map/pallas_call | solution.py:155
  (71 shorter events, 5.3 us)
Async XLA Ops:
  0.0 103.3 %copy-start = (bf16[256,256]{1,0:T(8,128)(2,1)S(1)}, bf16[256,256]{1,0:T(8,128)(2,1)}, u32[]{:S(2)}) copy-start(bf16[256,256]{1,0:T(8,128)(2,1)} %param.20) | copy-start | bytes 393220
  86.0 10.0 %copy-start.1 = (bf16[3,256,256]{2,1,0:T(8,128)(2,1)S(1)}, bf16[3,256,256]{2,1,0:T(8,128)(2,1)}, u32[]{:S(2)}) copy-start(bf16[3,256,256]{2,1,0:T(8,128)(2,1)} %param.19) | copy-start | bytes 1179652
  96.3 5.3 %collective-permute-start = (bf16[2,1,128,256]{3,2,1,0:T(8,128)(2,1)S(1)}, bf16[2,1,128,256]{3,2,1,0:T(8,128)(2,1)S(1)}, u32[]{:S(2)}, u32[]{:S(2)}) collective-permute-start(bf16[2,1,128,256]{3,2,1,0:T(8,128)(2,1)S(1)} %pad_maximum_fusion.2), channel_id=1, source_target_pairs={{0,1},{1,0},{2,3},{3,2},{4,5},{5,4},{6,7},{7,6},{8,9},{9,8},{10,11... | collective-permute-start | bytes 393224 | tf_op jit(solution)/shard_map/ppermute | solution.py:211
  104.5 6.7 %collective-permute-start.1 = (bf16[2,1,128,256]{3,2,1,0:T(8,128)(2,1)S(1)}, bf16[2,1,128,256]{3,2,1,0:T(8,128)(2,1)S(1)}, u32[]{:S(2)}, u32[]{:S(2)}) collective-permute-start(bf16[2,1,128,256]{3,2,1,0:T(8,128)(2,1)S(1)} %pad_maximum_fusion.3), channel_id=1, source_target_pairs={{0,2},{1,3},{2,0},{3,1},{4,6},{5,7},{6,4},{7,5},{8,10},{9,11},{10,... | collective-permute-start | bytes 393224 | tf_op jit(solution)/shard_map/ppermute | solution.py:211
  114.1 5.1 %collective-permute-start.2 = (bf16[2,1,128,256]{3,2,1,0:T(8,128)(2,1)S(1)}, bf16[2,1,128,256]{3,2,1,0:T(8,128)(2,1)S(1)}, u32[]{:S(2)}, u32[]{:S(2)}) collective-permute-start(bf16[2,1,128,256]{3,2,1,0:T(8,128)(2,1)S(1)} %pad_maximum_fusion.4), channel_id=1, source_target_pairs={{0,4},{1,5},{2,6},{3,7},{4,0},{5,1},{6,2},{7,3},{8,12},{9,13},{10,... | collective-permute-start | bytes 393224 | tf_op jit(solution)/shard_map/ppermute | solution.py:211
  122.2 5.0 %collective-permute-start.3 = (bf16[2,1,128,256]{3,2,1,0:T(8,128)(2,1)S(1)}, bf16[2,1,128,256]{3,2,1,0:T(8,128)(2,1)S(1)}, u32[]{:S(2)}, u32[]{:S(2)}) collective-permute-start(bf16[2,1,128,256]{3,2,1,0:T(8,128)(2,1)S(1)} %pad_maximum_fusion.5), channel_id=1, source_target_pairs={{0,8},{1,9},{2,10},{3,11},{4,12},{5,13},{6,14},{7,15},{8,0},{9,1},... | collective-permute-start | bytes 393224 | tf_op jit(solution)/shard_map/ppermute | solution.py:211
  130.1 6.6 %collective-permute-start.4 = (bf16[2,1,128,256]{3,2,1,0:T(8,128)(2,1)S(1)}, bf16[2,1,128,256]{3,2,1,0:T(8,128)(2,1)S(1)}, u32[]{:S(2)}, u32[]{:S(2)}) collective-permute-start(bf16[2,1,128,256]{3,2,1,0:T(8,128)(2,1)S(1)} %pad_maximum_fusion.6), channel_id=1, source_target_pairs={{0,16},{1,17},{2,18},{3,19},{4,20},{5,21},{6,22},{7,23},{8,24},{9,... | collective-permute-start | bytes 393224 | tf_op jit(solution)/shard_map/ppermute | solution.py:211
  139.2 5.8 %collective-permute-start.5 = (bf16[128,256]{1,0:T(8,128)(2,1)S(1)}, bf16[128,256]{1,0:T(8,128)(2,1)S(1)}, u32[]{:S(2)}, u32[]{:S(2)}) collective-permute-start(bf16[128,256]{1,0:T(8,128)(2,1)S(1)} %get-tuple-element.6), channel_id=1, source_target_pairs={{0,2},{1,3},{2,0},{3,1},{4,6},{5,7},{6,4},{7,5},{8,10},{9,11},{10,... | collective-permute-start | bytes 196616 | tf_op jit(solution)/shard_map/ppermute | solution.py:211
  145.0 6.6 %collective-permute-start.6 = (bf16[256,256]{1,0:T(8,128)(2,1)S(1)}, bf16[256,256]{1,0:T(8,128)(2,1)S(1)}, u32[]{:S(2)}, u32[]{:S(2)}) collective-permute-start(bf16[256,256]{1,0:T(8,128)(2,1)S(1)} %pad_maximum_fusion.7), channel_id=1, source_target_pairs={{0,16},{1,17},{2,18},{3,19},{4,20},{5,21},{6,22},{7,23},{8,24},{9,... | collective-permute-start | bytes 393224 | tf_op jit(solution)/shard_map/ppermute | solution.py:211
  151.6 6.5 %collective-permute-start.7 = (bf16[512,256]{1,0:T(8,128)(2,1)S(1)}, bf16[512,256]{1,0:T(8,128)(2,1)S(1)}, u32[]{:S(2)}, u32[]{:S(2)}) collective-permute-start(bf16[512,256]{1,0:T(8,128)(2,1)S(1)} %pad_maximum_fusion.1), channel_id=1, source_target_pairs={{0,1},{1,0},{2,3},{3,2},{4,5},{5,4},{6,7},{7,6},{8,9},{9,8},{10,11... | collective-permute-start | bytes 786440 | tf_op jit(solution)/shard_map/ppermute | solution.py:211
  158.1 9.3 %collective-permute-start.8 = (bf16[1024,256]{1,0:T(8,128)(2,1)S(1)}, bf16[1024,256]{1,0:T(8,128)(2,1)S(1)}, u32[]{:S(2)}, u32[]{:S(2)}) collective-permute-start(bf16[1024,256]{1,0:T(8,128)(2,1)S(1)} %pad_maximum_fusion), channel_id=1, source_target_pairs={{0,4},{1,5},{2,6},{3,7},{4,0},{5,1},{6,2},{7,3},{8,12},{9,13},{10,... | collective-permute-start | bytes 1572872 | tf_op jit(solution)/shard_map/ppermute | solution.py:211
  168.2 44.5 %collective-permute-start.9 = (bf16[2048,256]{1,0:T(8,128)(2,1)}, bf16[2048,256]{1,0:T(8,128)(2,1)S(1)}, u32[]{:S(2)}, u32[]{:S(2)}) collective-permute-start(bf16[2048,256]{1,0:T(8,128)(2,1)} %get-tuple-element.7), channel_id=1, source_target_pairs={{0,8},{1,9},{2,10},{3,11},{4,12},{5,13},{6,14},{7,15},{8,0},{9,1},... | collective-permute-start | bytes 3145736 | tf_op jit(solution)/shard_map/ppermute | solution.py:211
  212.8 1.3 copy-start.2
